TPU v7x, 512 devices: a whole 4x4x16 slice. The times are simulated.
512 devices in a mesh: group: 8 (over x, core), dev: 64 (over y, z).
Axes of the slice: x: 4, y: 4, z: 16, core: 2. Of those that a mesh axis runs over, the one named last changes fastest.
Arguments:
- probes: bfloat16 [2048, 32, 1024], P(('group', 'dev')), may hold values from -6 to 6
- points: float32 [2048, 3, 1024], P(('group', 'dev')), may hold values from -2.5 to 5.5
- leaf_order: int32 [2048, 1024], P(('group', 'dev')), may hold values from 0 to 1023, each once within a row
- leaf_basis: bfloat16 [2048, 1024, 256], P(('group', 'dev')), may hold values from -0.1875 to 0.1875
- node_transfer: bfloat16 [512, 4, 256, 256], P(('group', 'dev')), may hold values from -0.375 to 0.375
- group_transfer: bfloat16 [512, 256, 256], P(('group', 'dev')), may hold values from -0.375 to 0.375
- node_skeleton: float32 [512, 3, 256], P('group'), may hold values from 0 to 2
- group_skeleton: float32 [8, 3, 256], replicated, may hold values from 0 to 8
- near_pattern: int32 [2048, 5], P(('group', 'dev')), may hold values from 0 to 1, as said below
- node_coupling: int32 [512, 9], P(('group', 'dev')), may hold values 0 or 1
- signal_variance: float32 [], replicated, may hold values from 0.1 to 0.25
- noise_variance: float32 [], replicated, may hold values from 0.5 to 1.5
Outputs:
- applied: bfloat16 [2048, 32, 1024], P(('group', 'dev'))
Inputs may be any that keep to these rules, and one draw needn't show every extreme that they name: `leaf_order`: each row is a permutation. `near_pattern`: 1 marks a near-field block with the leaf at that offset; entries for leaves outside the set are not used. `node_coupling`: 1 marks a coupling with the node at that offset; entries with offsets under 2 or nodes outside the subtree are not used.
All inputs are finite; a program needn't handle non-finite values. No bound on the sum of `node_coupling` on one device may be relied on, other than what follows from the above.
Results may differ from a plain program's by a relative error of at most 0.012.
Values may be sent and summed in bfloat16 or wider, within the bound.
No kernel may reach another device: no remote copies, remote signals or barrier semaphores. Data moves between devices by JAX's collectives and lax.ppermute only.
A program may use at most 64 MiB of HBM per device.

v0:
```python
import jax
import jax.numpy as jnp
from jax import lax
from jax.sharding import Mesh
from jax.sharding import PartitionSpec as P

NEAR_REACH = 2
COUPLE_REACH = 4
GROUP_DEV = ("group", "dev_0", "dev_1", "dev_2")
DEV = ("dev_0", "dev_1", "dev_2")


ROOT_THREE = 1.7320508075688772
LENGTH_SCALE = 0.5


def with_halo(value, axis, width):
    peers, length = (lax.axis_size(axis), value.shape[0])
    up = [(i, i + 1) for i in range(peers - 1)]
    leading = value[:width]
    return lax.ppermute(leading, axis, [(b, a) for a, b in up])


def spread_out(value, high, width):
    pieces = [value[i] for i in range(value.shape[0])] + [high[i] for i in range(high.shape[0])]
    return dict(enumerate(pieces, start=width))


def from_behind(block, axis, distance):
    devices = range(lax.axis_size(axis))
    route = [(i - distance, i) for i in devices if i - distance in devices]
    return lax.ppermute(block, axis, route)


def tree_sum(value, axis):
    peers = lax.axis_size(axis)
    step = 1
    while step < peers:
        value = value + lax.ppermute(value, axis, [(i, i ^ step) for i in range(peers)])
        step *= 2
    return value


def from_everyone(value, axis):
    peers = lax.axis_size(axis)
    return lax.all_to_all(
        jnp.broadcast_to(value[None], (peers, *value.shape)), axis, 0, 0, tiled=True
    )


def cyclic_from_behind(block, axis, distance):
    peers = lax.axis_size(axis)
    return lax.ppermute(block, axis, [(i, (i + distance) % peers) for i in range(peers)])


def matern(source, target, amplitude):
    square = (source[0][:, None] - target[0][None, :]) ** 2
    square = square + (source[1][:, None] - target[1][None, :]) ** 2
    square = square + (source[2][:, None] - target[2][None, :]) ** 2
    scaled = jnp.sqrt(square) * (ROOT_THREE / LENGTH_SCALE)
    return (amplitude * (1.0 + scaled) * jnp.exp(-scaled)).astype(jnp.bfloat16)


def one_hot(ordering, size):
    rows = lax.broadcasted_iota(jnp.int32, (size, size), 0)
    return (rows == ordering[None, :]).astype(jnp.bfloat16)


def on_device(
    probes,
    points,
    leaf_order,
    leaf_basis,
    node_transfer,
    group_transfer,
    node_skeleton,
    group_skeleton,
    near_pattern,
    node_coupling,
    signal_variance,
    noise_variance,
):
    leaf_count, probe_count, leaf_size = probes.shape
    skeleton = leaf_basis.shape[2]
    f32 = jnp.float32

    hots = jax.vmap(lambda ordering: one_hot(ordering, leaf_size))(leaf_order)
    ordered = lax.dot_general(
        probes, hots, (((2,), (1,)), ((0,), (0,))), preferred_element_type=f32
    ).astype(jnp.bfloat16)

    leaf_coef = lax.dot_general(
        ordered, leaf_basis, (((2,), (1,)), ((0,), (0,))), preferred_element_type=f32
    ).astype(jnp.bfloat16)
    stacked = leaf_coef.transpose(1, 0, 2).reshape(probe_count, leaf_count * skeleton)
    transfer_flat = node_transfer[0].reshape(leaf_count * skeleton, skeleton)
    node_coef = jnp.dot(stacked, transfer_flat, preferred_element_type=f32).astype(jnp.bfloat16)
    group_term = jnp.dot(node_coef, group_transfer[0], preferred_element_type=f32)
    node_index = lax.axis_index(DEV)
    node_total = lax.axis_size(DEV)

    probes_halo = with_halo(ordered, GROUP_DEV, NEAR_REACH)
    points_halo = with_halo(points, GROUP_DEV, NEAR_REACH)
    wide = leaf_count + 2 * NEAR_REACH
    own = range(NEAR_REACH, NEAR_REACH + leaf_count)
    pattern = near_pattern.astype(f32)
    jobs = [(b, b) for b in own]
    cross, inner = [], []
    for gap in range(1, NEAR_REACH + 1):
        for a in range(wide - gap):
            b = a + gap
            if a in own and b in own:
                inner.append((a, b))
            elif a in own:
                cross.append((a, b))
    jobs += cross + inner
    near = [jnp.zeros((probe_count, leaf_size), f32) for _ in range(leaf_count)]
    outgoing = {}

    def run_job(job, at, values):
        a, b = job
        tile = lax.optimization_barrier(matern(at[a], at[b], signal_variance))
        if a == b:
            t = b - NEAR_REACH
            near[t] = near[t] + jnp.dot(values[b], tile, preferred_element_type=f32) * pattern[
                t, NEAR_REACH
            ]
            return
        gap = b - a
        if b in own:
            t = b - NEAR_REACH
            near[t] = near[t] + jnp.dot(
                values[a], tile, preferred_element_type=f32
            ) * pattern[t, NEAR_REACH - gap]
        if a in own:
            t = a - NEAR_REACH
            near[t] = near[t] + lax.dot_general(
                values[b], tile, (((1,), (1,)), ((), ())), preferred_element_type=f32
            ) * pattern[t, NEAR_REACH + gap]
        if b not in own:
            outgoing[job] = jnp.dot(values[a], tile, preferred_element_type=f32)

    rounds = ["dev_1", "dev_2", "dev_0"]
    steps = len(rounds) + 1
    running = group_term
    extra = node_coef.astype(f32)[None]
    block = lax.axis_size("dev_2")
    row = block * lax.axis_size("dev_1")
    group_index = lax.axis_index("group")
    group_total = lax.axis_size("group")
    for step in range(steps):
        chunk = jobs[step * len(jobs) // steps : (step + 1) * len(jobs) // steps]
        if any(job in cross for job in chunk):
            running, extra, points_of, probes_of, points_halo, probes_halo = (
                lax.optimization_barrier(
                    (running, extra, points, ordered, points_halo, probes_halo)
                )
            )
            at = spread_out(points_of, points_halo, NEAR_REACH)
            values = spread_out(probes_of, probes_halo, NEAR_REACH)
        else:
            running, extra, at, values = lax.optimization_barrier((running, extra, points, ordered))
            at = {b: at[b - NEAR_REACH] for b in own}
            values = {b: values[b - NEAR_REACH] for b in own}
        if step < len(rounds):
            received = from_everyone(jnp.concatenate([running[None], extra]), rounds[step])
        else:
            own_coef = running.astype(jnp.bfloat16)
            group_coef = from_everyone(own_coef, "group")
        for job in chunk:
            run_job(job, at, values)
        if step < len(rounds):
            running = jnp.sum(received[:, 0], axis=0)
            if step == 0:
                extra = received[:, 1]
            elif step == 1:
                row_coef = received[:, 1:].transpose(1, 0, 2, 3).reshape(row, probe_count, skeleton)
                extra = jnp.concatenate([row_coef[:COUPLE_REACH], row_coef[row - COUPLE_REACH :]])
            else:
                ends_coef = received[:, 1:]
    incoming = lax.ppermute(
        jnp.stack([outgoing[job] for job in cross]),
        GROUP_DEV,
        [(i, i + 1) for i in range(lax.axis_size(GROUP_DEV) - 1)],
    )
    for k, (a, b) in enumerate(cross):
        t = b - NEAR_REACH - leaf_count
        near[t] = near[t] + incoming[k] * pattern[t, NEAR_REACH - (b - a)]
    near = jnp.stack(near)

    own_skeleton = lax.dynamic_index_in_dim(group_skeleton, group_index, 0, keepdims=False)
    group_tiles = matern(
        group_skeleton.transpose(1, 0, 2).reshape(3, group_total * skeleton),
        own_skeleton,
        signal_variance,
    )
    others = lax.broadcasted_iota(jnp.int32, (group_total, 1, 1), 0) != group_index
    group_stack = jnp.where(others, group_coef, jnp.zeros_like(group_coef))
    group_stack = group_stack.transpose(1, 0, 2).reshape(probe_count, group_total * skeleton)
    far_group = jnp.dot(group_stack, group_tiles, preferred_element_type=f32)
    group_local = far_group.astype(jnp.bfloat16)

    own_node = lax.dynamic_index_in_dim(node_skeleton, node_index, 0, keepdims=False)
    ends = ends_coef.shape[1]
    table = jnp.concatenate([row_coef, ends_coef.reshape(-1, probe_count, skeleton)])
    line = node_index // row
    lines = lax.axis_size("dev_0")
    partner_points, picks, usable = [], [], []
    for offset in range(-COUPLE_REACH, COUPLE_REACH + 1):
        if abs(offset) < 2:
            continue
        partner = node_index + offset
        usable.append(
            (partner >= 0) & (partner < node_total) & (node_coupling[0, offset + COUPLE_REACH] > 0)
        )
        clamped = jnp.clip(partner, 0, node_total - 1)
        partner_points.append(lax.dynamic_index_in_dim(node_skeleton, clamped, 0, keepdims=False))
        along = node_index % row + offset
        same = jnp.clip(along, 0, row - 1)
        below = row + jnp.clip(line - 1, 0, lines - 1) * ends + COUPLE_REACH
        below = below + jnp.clip(along + COUPLE_REACH, 0, COUPLE_REACH - 1)
        above = row + jnp.clip(line + 1, 0, lines - 1) * ends
        above = above + jnp.clip(along - row, 0, COUPLE_REACH - 1)
        picks.append(jnp.where(along < 0, below, jnp.where(along >= row, above, same)))
    picked = jnp.take(table, jnp.stack(picks), axis=0)
    picked = jnp.where(jnp.stack(usable)[:, None, None], picked, jnp.zeros_like(picked))
    picked = picked.astype(jnp.bfloat16).transpose(1, 0, 2).reshape(probe_count, -1)
    couple_tiles = matern(jnp.concatenate(partner_points, axis=1), own_node, signal_variance)
    far_node = jnp.dot(picked, couple_tiles, preferred_element_type=f32)

    pushed = lax.dot_general(
        group_local, group_transfer[0], (((1,), (1,)), ((), ())), preferred_element_type=f32
    )
    node_local = (pushed + far_node).astype(jnp.bfloat16)
    spread = lax.dot_general(
        node_local, transfer_flat, (((1,), (1,)), ((), ())), preferred_element_type=f32
    )
    leaf_local = (
        spread.reshape(probe_count, leaf_count, skeleton).transpose(1, 0, 2).astype(jnp.bfloat16)
    )
    far_leaf = lax.dot_general(
        leaf_local, leaf_basis, (((2,), (2,)), ((0,), (0,))), preferred_element_type=f32
    )
    result = (far_leaf + near + noise_variance * ordered.astype(f32)).astype(jnp.bfloat16)
    restored = lax.dot_general(
        result, hots, (((2,), (2,)), ((0,), (0,))), preferred_element_type=f32
    )
    return restored.astype(jnp.bfloat16)


def solution(mesh):
    finer = Mesh(mesh.devices.reshape(mesh.shape["group"], 4, 4, 4), GROUP_DEV)
    return jax.shard_map(
        on_device,
        mesh=finer,
        in_specs=(
            P(GROUP_DEV, None, None),
            P(GROUP_DEV, None, None),
            P(GROUP_DEV, None),
            P(GROUP_DEV, None, None),
            P(GROUP_DEV, None, None, None),
            P(GROUP_DEV, None, None),
            P("group", None, None),
            P(),
            P(GROUP_DEV, None),
            P(GROUP_DEV, None),
            P(),
            P(),
        ),
        out_specs=P(GROUP_DEV, None, None),
        check_vma=False,
    )
```

profile of v0, /device:TPU:1, one launch (start us, length us, event | category | flops | bytes accessed | tf_op | source)
XLA Modules:
  0.0 166.2 jit_solution(1418626566800620158)
XLA Ops:
  0.0 1.0 slice.482
  1.0 15.0 %collective-permute-start = (f32[2,3,1024]{2,0,1:T(2,128)S(1)}, f32[2,3,1024]{2,0,1:T(2,128)}, u32[]{:S(2)}, u32[]{:S(2)}) collective-permute-start(f32[2,3,1024]{2,0,1:T(2,128)S(1)} %slice.482), channel_id=1, source_target_pairs={{1,0},{2,1},{3,2},{4,3},{5,4},{6,5},{7,6},{8,7},{9,8},{10,9},{11,1... | collective-permute-start | bytes 73736 | tf_op jit(solution)/shard_map/ppermute | solution.py:21
  15.9 3.9 %fusion.6 = bf16[4,1024,32]{1,2,0:T(8,128)(2,1)S(1)} fusion(bf16[4,32,1024]{2,1,0:T(8,128)(2,1)} %param.12, s32[4,1024]{1,0:T(4,128)} %param.14), kind=kOutput, calls=%fused_computation.24 | convolution fusion | flops 272760832 | bytes 540672 | tf_op jit(solution)/shard_map/dot_general | solution.py:88
  19.9 0.7 slice.597
  20.6 3.0 %collective-permute-start.1 = (bf16[2,32,1024]{2,1,0:T(8,128)(2,1)}, bf16[2,32,1024]{2,1,0:T(8,128)(2,1)S(1)}, u32[]{:S(2)}, u32[]{:S(2)}) collective-permute-start(bf16[2,32,1024]{2,1,0:T(8,128)(2,1)} %slice.597), channel_id=1, source_target_pairs={{1,0},{2,1},{3,2},{4,3},{5,4},{6,5},{7,6},{8,7},{9,8},{10,9},{11,1... | collective-permute-start | bytes 393224 | tf_op jit(solution)/shard_map/ppermute | solution.py:21
  24.5 0.7 broadcast_in_dim.78
  25.2 3.4 %all-to-all-start = ((f32[4,2,32,256]{3,2,1,0:T(8,128)}), f32[4,2,32,256]{3,2,1,0:T(8,128)S(1)}, u32[]{:S(2)}, u32[]{:S(2)}) async-start(f32[4,2,32,256]{3,2,1,0:T(8,128)} %broadcast_in_dim.78), calls=%async_computation | async-start | bytes 524288 | tf_op jit(solution)/shard_map/all_to_all | solution.py:46
  28.8 0.6 iota_compare_fusion.7
  29.4 0.7 slice.514
  30.0 0.7 fusion.123
  32.3 0.7 fusion.124
  36.9 0.6 pad_clamp_fusion
  37.5 1.1 constant_dynamic-slice_fusion.5
  38.7 0.6 slice_reduce_fusion.5
  39.3 0.6 copy.32
  40.0 4.3 %multiply_convert_fusion.11 = bf16[1024,1024]{1,0:T(8,128)(2,1)} fusion(f32[1024]{0:T(1024)S(1)} %bitcast.362, f32[1024]{0:T(1024)S(1)} %bitcast.363, f32[1024]{0:T(1024)S(1)} %bitcast.361, f32[]{:T(128)S(6)} %copy.46), kind=kLoop, calls=%fused_computation.17 | loop fusion | flops 14680064 | bytes 2109444 | tf_op jit(solution)/shard_map/convert_element_type | solution.py:61
  44.2 7.6 %multiply_convert_fusion.2 = (bf16[1024,1024]{1,0:T(8,128)(2,1)}, bf16[1024,1024]{1,0:T(8,128)(2,1)}) fusion(f32[1024]{0:T(1024)S(1)} %bitcast.346, f32[1024]{0:T(1024)S(1)} %bitcast.347, f32[1024]{0:T(1024)S(1)} %bitcast.348, f32[]{:T(128)S(6)} %copy.46, f32[1024]{0:T(1024)S(1)} %bitcast.349, f32[1024]{0:T(1024)S(1)} %bitcast.350, f32[1024]{0:T(1024)S(1)} %bitcast.351), kind=kLoop, calls=%fused_computation.8 | loop fusion | flops 29360128 | bytes 4218884 | tf_op jit(solution)/shard_map/convert_element_type | solution.py:61
  51.8 3.4 %convolution_multiply_fusion.16 = f32[32,1024]{1,0:T(8,128)} fusion(bf16[1024,1024]{1,0:T(8,128)(2,1)} %multiply_convert_fusion.11, f32[]{:T(128)} %bitcast.55, bf16[4,32,1024]{2,1,0:T(8,128)(2,1)S(1)} %bitcast.289), kind=kOutput, calls=%fused_computation.60 | convolution fusion | flops 67141632 | bytes 2293764 | tf_op jit(solution)/shard_map/dot_general | solution.py:125
  55.2 1.3 constant_dynamic-slice_fusion.1
  56.7 0.7 stack.89
  57.3 0.5 compare_and_fusion
  57.9 3.4 %convolution_multiply_fusion.9 = f32[32,1024]{1,0:T(8,128)} fusion(bf16[1024,1024]{1,0:T(8,128)(2,1)} %get-tuple-element.154, f32[]{:T(128)} %bitcast.125, bf16[4,32,1024]{2,1,0:T(8,128)(2,1)S(1)} %bitcast.290), kind=kOutput, calls=%fused_computation.48 | convolution fusion | flops 67141632 | bytes 2293764 | tf_op jit(solution)/shard_map/dot_general | solution.py:125
  61.3 1.7 %convolution_multiply_fusion.13 = f32[32,1024]{1,0:T(8,128)} fusion(bf16[1024,1024]{1,0:T(8,128)(2,1)S(1)} %copy-done.4, f32[]{:T(128)} %bitcast.102, bf16[4,32,1024]{2,1,0:T(8,128)(2,1)S(1)} %bitcast.291), kind=kOutput, calls=%fused_computation.55 | convolution fusion | flops 67141632 | bytes 2293764 | tf_op jit(solution)/shard_map/dot_general | solution.py:125
  63.1 0.9 broadcast_in_dim.80
  64.0 3.7 %all-to-all-start.1 = ((f32[4,5,32,256]{3,2,1,0:T(8,128)}), f32[4,5,32,256]{3,2,1,0:T(8,128)S(1)}, u32[]{:S(2)}, u32[]{:S(2)}) async-start(f32[4,5,32,256]{3,2,1,0:T(8,128)} %broadcast_in_dim.80), calls=%async_computation.1 | async-start | bytes 1310720 | tf_op jit(solution)/shard_map/all_to_all | solution.py:46
  67.7 0.9 fusion.120
  68.5 10.0 %multiply_convert_fusion.7 = (bf16[1024,1024]{1,0:T(8,128)(2,1)S(1)}, bf16[1024,1024]{1,0:T(8,128)(2,1)S(1)}, bf16[1024,1024]{1,0:T(8,128)(2,1)S(1)}) fusion(f32[1024]{0:T(1024)S(1)} %bitcast.353, f32[1024]{0:T(1024)S(1)} %bitcast.354, f32[1024]{0:T(1024)S(1)} %bitcast.352, f32[1024]{0:T(1024)S(1)} %bitcast.359, f32[1024]{0:T(1024)S(1)} %bitcast.358, ...), kind=kLoop, calls=%fused_computation.13 | loop fusion | flops 44040192 | bytes 6328324 | tf_op jit(solution)/shard_map/convert_element_type | solution.py:61
  78.6 1.1 convolution_bitcast_fusion.1
  79.7 1.1 convolution_bitcast_fusion.2
  80.9 1.1 convolution_multiply_fusion.4
  82.0 2.0 %fusion.17 = f32[32,1024]{1,0:T(8,128)} fusion(f32[32,1024]{1,0:T(8,128)S(1)} %copy-done.12, bf16[1024,1024]{1,0:T(8,128)(2,1)S(1)} %get-tuple-element.115, f32[]{:T(128)} %bitcast.127, bf16[2,32,1024]{2,1,0:T(8,128)(2,1)S(1)} %copy-done.20), kind=kOutput, calls=%fused_computation.47 | convolution fusion | flops 67174400 | bytes 2424836 | tf_op jit(solution)/shard_map/dot_general | solution.py:137
  84.0 1.9 %fusion.12 = f32[32,1024]{1,0:T(8,128)} fusion(f32[32,1024]{1,0:T(8,128)S(1)} %convolution_multiply_fusion.4, bf16[1024,1024]{1,0:T(8,128)(2,1)S(1)} %get-tuple-element.116, f32[]{:T(128)} %bitcast.134, bf16[2,32,1024]{2,1,0:T(8,128)(2,1)S(1)} %copy-done.20), kind=kOutput, calls=%fused_computation.37 | convolution fusion | flops 67174400 | bytes 2424836 | tf_op jit(solution)/shard_map/dot_general | solution.py:137
  86.1 1.2 broadcast_in_dim.82
  87.3 4.3 %all-to-all-start.2 = ((f32[4,9,32,256]{3,2,1,0:T(8,128)}), f32[4,9,32,256]{3,2,1,0:T(8,128)}, u32[]{:S(2)}, u32[]{:S(2)}) async-start(f32[4,9,32,256]{3,2,1,0:T(8,128)} %broadcast_in_dim.82), calls=%async_computation.2 | async-start | bytes 2359296 | tf_op jit(solution)/shard_map/all_to_all | solution.py:46
  91.6 1.0 fusion.118
  92.6 3.3 %multiply_convert_fusion.6 = bf16[1024,1024]{1,0:T(8,128)(2,1)S(1)} fusion(f32[1024]{0:T(1024)S(1)} %bitcast.344, f32[1024]{0:T(1024)S(1)} %bitcast.340, f32[1024]{0:T(1024)S(1)} %bitcast.343, f32[1024]{0:T(1024)S(1)} %bitcast.341, f32[1024]{0:T(1024)S(1)} %bitcast.345, f32[1024]{0:T(1024)S(1)} %bitcast.342, f32[]{:T(128)S(6)} %copy.46), kind=kLoop, calls=%fused_computation.12 | loop fusion | flops 14680064 | bytes 2121732 | tf_op jit(solution)/shard_map/convert_element_type | solution.py:61
  95.9 6.7 %multiply_convert_fusion.10 = (bf16[1024,1024]{1,0:T(8,128)(2,1)S(1)}, bf16[1024,1024]{1,0:T(8,128)(2,1)S(1)}) fusion(f32[1024]{0:T(1024)S(1)} %bitcast.335, f32[1024]{0:T(1024)S(1)} %bitcast.336, f32[1024]{0:T(1024)S(1)} %bitcast.337, f32[1024]{0:T(1024)S(1)} %bitcast.338, f32[1024]{0:T(1024)S(1)} %bitcast.339, f32[1024]{0:T(1024)S(1)} %bitcast.331, ...), kind=kLoop, calls=%fused_computation.16 | loop fusion | flops 29360128 | bytes 4231172 | tf_op jit(solution)/shard_map/convert_element_type | solution.py:61
  103.5 0.8 pad_maximum_fusion.1
  104.3 3.1 %collective-permute-start.2 = (f32[3,32,1024]{2,1,0:T(8,128)}, f32[3,32,1024]{2,1,0:T(8,128)}, u32[]{:S(2)}, u32[]{:S(2)}) collective-permute-start(f32[3,32,1024]{2,1,0:T(8,128)} %pad_maximum_fusion.1), channel_id=1, source_target_pairs={{0,1},{1,2},{2,3},{3,4},{4,5},{5,6},{6,7},{7,8},{8,9},{9,10},{10,1... | collective-permute-start | bytes 1179656 | tf_op jit(solution)/shard_map/ppermute | solution.py:181
  107.5 1.9 %fusion.22 = f32[32,1024]{1,0:T(8,128)} fusion(f32[32,1024]{1,0:T(8,128)S(1)} %copy-done.10, bf16[1024,1024]{1,0:T(8,128)(2,1)S(1)} %get-tuple-element.110, f32[]{:T(128)} %bitcast.63, bf16[4,32,1024]{2,1,0:T(8,128)(2,1)S(1)} %bitcast.296), kind=kOutput, calls=%fused_computation.59 | convolution fusion | flops 67174400 | bytes 2424836 | tf_op jit(solution)/shard_map/dot_general | solution.py:137
  109.4 1.2 fusion.20
  110.7 1.4 fusion.19
  112.2 1.7 %fusion.16 = f32[32,1024]{1,0:T(8,128)} fusion(f32[32,1024]{1,0:T(8,128)S(1)} %copy-done.16, bf16[1024,1024]{1,0:T(8,128)(2,1)S(1)} %get-tuple-element.111, f32[]{:T(128)} %bitcast.128, bf16[4,32,1024]{2,1,0:T(8,128)(2,1)S(1)} %bitcast.299), kind=kOutput, calls=%fused_computation.45 | convolution fusion | flops 67174400 | bytes 2424836 | tf_op jit(solution)/shard_map/dot_general | solution.py:132
  113.9 1.9 %fusion.11 = f32[32,1024]{1,0:T(8,128)} fusion(f32[32,1024]{1,0:T(8,128)S(1)} %copy-done.15, bf16[1024,1024]{1,0:T(8,128)(2,1)S(1)} %multiply_convert_fusion.6, f32[]{:T(128)} %bitcast.136, bf16[2,32,1024]{2,1,0:T(8,128)(2,1)S(1)} %copy-done.21), kind=kOutput, calls=%fused_computation.35 | convolution fusion | flops 67174400 | bytes 2424836 | tf_op jit(solution)/shard_map/dot_general | solution.py:137
  115.8 0.9 slice_reduce_fusion
  116.8 0.7 broadcast_in_dim.83
  117.4 5.7 %all-to-all-start.3 = ((bf16[8,32,256]{2,1,0:T(8,128)(2,1)}), bf16[8,32,256]{2,1,0:T(8,128)(2,1)S(1)}, u32[]{:S(2)}, u32[]{:S(2)}) async-start(bf16[8,32,256]{2,1,0:T(8,128)(2,1)} %broadcast_in_dim.83), calls=%async_computation.3 | async-start | bytes 262144 | tf_op jit(solution)/shard_map/all_to_all | solution.py:46
  123.2 10.5 %multiply_convert_fusion.9 = (bf16[1024,1024]{1,0:T(8,128)(2,1)}, bf16[1024,1024]{1,0:T(8,128)(2,1)}, bf16[1024,1024]{1,0:T(8,128)(2,1)}) fusion(f32[1024]{0:T(1024)S(1)} %bitcast.326, f32[1024]{0:T(1024)S(1)} %bitcast.327, f32[1024]{0:T(1024)S(1)} %bitcast.328, f32[1024]{0:T(1024)S(1)} %bitcast.329, f32[1024]{0:T(1024)S(1)} %bitcast.330, ...), kind=kLoop, calls=%fused_computation.15 | loop fusion | flops 44040192 | bytes 6340612 | tf_op jit(solution)/shard_map/convert_element_type | solution.py:61
  133.6 1.3 slice.606
  135.0 1.0 pad_maximum_fusion
  135.9 1.8 %gather_fusion = bf16[6,32,256]{2,1,0:T(8,128)(2,1)S(1)} fusion(bf16[48,32,256]{2,1,0:T(8,128)(2,1)} %pad_maximum_fusion, s32[1024]{0:T(1024)} %pad_clamp_fusion), kind=kCustom, calls=%fused_computation | custom fusion | bytes 196632 | tf_op jit(solution)/shard_map/jit(_take)/gather | solution.py:225
  137.8 0.9 fusion.65
  138.7 3.1 %fusion.15 = f32[32,1024]{1,0:T(8,128)S(1)} fusion(f32[32,1024]{1,0:T(8,128)S(1)} %copy-done.18, bf16[1024,1024]{1,0:T(8,128)(2,1)} %get-tuple-element.113, f32[]{:T(128)} %bitcast.129, bf16[4,32,1024]{2,1,0:T(8,128)(2,1)S(1)} %bitcast.300), kind=kOutput, calls=%fused_computation.43 | convolution fusion | flops 67174400 | bytes 2424836 | tf_op jit(solution)/shard_map/dot_general | solution.py:137
  141.8 1.1 fusion.14
  143.0 0.6 copy.30
  143.6 1.3 fusion.10
  144.9 4.2 %fusion.59 = f32[1,32,1024]{2,1,0:T(8,128)} fusion(f32[3,32,1024]{2,1,0:T(8,128)} %collective-permute-done.2, f32[32,1024]{1,0:T(8,128)S(1)} %copy-done.14, bf16[1024,1024]{1,0:T(8,128)(2,1)S(1)} %copy-done.2, f32[]{:T(128)} %bitcast.95, f32[]{:T(128)} %bitcast.93, f32[]{:T(128)} %bitcast.71, bf16[4,32,1024]{2,1,0:T(8,128)(2,1)S(1)} %bitcast.303), kind=kOutput, calls=%fused_computation.100 | convolution fusion | flops 67305472 | bytes 2686988 | tf_op jit(solution)/shard_map/dot_general | solution.py:137
  149.2 2.9 %fusion.56 = f32[1,32,1024]{2,1,0:T(8,128)S(1)} fusion(f32[3,32,1024]{2,1,0:T(8,128)} %collective-permute-done.2, f32[32,1024]{1,0:T(8,128)S(1)} %fusion.19, bf16[1024,1024]{1,0:T(8,128)(2,1)S(1)} %copy-done.1, f32[]{:T(128)} %bitcast.118, f32[]{:T(128)} %bitcast.117, bf16[4,32,1024]{2,1,0:T(8,128)(2,1)S(1)} %bitcast.304), kind=kOutput, calls=%fused_computation.96 | convolution fusion | flops 67239936 | bytes 2555912 | tf_op jit(solution)/shard_map/dot_general | solution.py:137
  152.1 1.1 fusion.9
  153.2 0.8 select_bitcast_fusion
  154.0 3.4 %fusion.26 = f32[32,256]{1,0:T(8,128)} fusion(bf16[32,2048]{1,0:T(8,128)(2,1)S(1)} %bitcast.311, f32[256]{0:T(256)} %bitcast.367, f32[2048]{0:T(1024)S(1)} %bitcast.317, f32[256]{0:T(256)} %bitcast.368, f32[2048]{0:T(1024)} %bitcast.318, f32[256]{0:T(256)} %bitcast.369, f32[2048]{0:T(1024)S(1)} %bitcast.316, f32[]{:T(128)S(6)} %copy.46, ...), kind=kOutput, calls=%fused_computation.69 | convolution fusion | flops 45096960 | bytes 322564 | tf_op jit(solution)/shard_map/dot_general | solution.py:231
  157.4 2.3 %fusion.27 = bf16[32,256,1]{1,0,2:T(8,128)(2,1)S(1)} fusion(f32[32,256]{1,0:T(8,128)} %fusion.26, bf16[32,1536]{1,0:T(8,128)(2,1)} %bitcast.314, f32[256]{0:T(256)} %bitcast.366, f32[1536]{0:T(1024)} %get-tuple-element.44, f32[256]{0:T(256)} %bitcast.365, f32[1536]{0:T(1024)} %get-tuple-element.45, f32[256]{0:T(256)} %bitcast.364, ...), kind=kOutput, calls=%fused_computation.70 | convolution fusion | flops 30687232 | bytes 168964 | tf_op jit(solution)/shard_map/dot_general | solution.py:229
  159.7 1.6 fusion.5
  161.3 4.9 %fusion.7 = bf16[4,32,1024]{2,1,0:T(8,128)(2,1)} fusion(bf16[4,32,1024]{2,1,0:T(8,128)(2,1)} %fusion.5, s32[4,1024]{1,0:T(4,128)S(1)} %copy-done.26), kind=kOutput, calls=%fused_computation.25 | convolution fusion | flops 272760832 | bytes 540672 | tf_op jit(solution)/shard_map/dot_general | solution.py:245
  (92 shorter events, 2.4 us)
Async XLA Ops:
  0.0 23.7 %copy-start = (bf16[4,1024,256]{2,1,0:T(8,128)(2,1)S(1)}, bf16[4,1024,256]{2,1,0:T(8,128)(2,1)}, u32[]{:S(2)}) copy-start(bf16[4,1024,256]{2,1,0:T(8,128)(2,1)} %param.15) | copy-start | bytes 6291460
  1.0 62.0 %collective-permute-start = (f32[2,3,1024]{2,0,1:T(2,128)S(1)}, f32[2,3,1024]{2,0,1:T(2,128)}, u32[]{:S(2)}, u32[]{:S(2)}) collective-permute-start(f32[2,3,1024]{2,0,1:T(2,128)S(1)} %slice.482), channel_id=1, source_target_pairs={{1,0},{2,1},{3,2},{4,3},{5,4},{6,5},{7,6},{8,7},{9,8},{10,9},{11,1... | collective-permute-start | bytes 73736 | tf_op jit(solution)/shard_map/ppermute | solution.py:21
  19.9 4.3 %copy-start.5 = (bf16[1,4,256,256]{3,2,1,0:T(8,128)(2,1)S(1)}, bf16[1,4,256,256]{3,2,1,0:T(8,128)(2,1)}, u32[]{:S(2)}) copy-start(bf16[1,4,256,256]{3,2,1,0:T(8,128)(2,1)} %param.16) | copy-start | bytes 1572868
  19.9 4.4 %copy-start.22 = (bf16[1,256,256]{2,1,0:T(8,128)(2,1)S(1)}, bf16[1,256,256]{2,1,0:T(8,128)(2,1)}, u32[]{:S(2)}) copy-start(bf16[1,256,256]{2,1,0:T(8,128)(2,1)} %param.17) | copy-start | bytes 393220
  20.6 8.8 %copy-start.25 = (s32[4,5]{1,0:T(4,128)S(1)}, s32[4,5]{1,0:T(4,128)}, u32[]{:S(2)}) copy-start(s32[4,5]{1,0:T(4,128)} %param.20) | copy-start | bytes 244
  20.6 11.7 %copy-start.24 = (s32[1,9]{1,0:T(1,128)S(1)}, s32[1,9]{1,0:T(1,128)}, u32[]{:S(2)}) copy-start(s32[1,9]{1,0:T(1,128)} %param.21) | copy-start | bytes 112
  20.6 18.7 %copy-start.23 = (f32[8,3,256]{2,0,1:T(8,128)S(1)}, f32[8,3,256]{2,0,1:T(8,128)}, u32[]{:S(2)}) copy-start(f32[8,3,256]{2,0,1:T(8,128)} %param.19) | copy-start | bytes 73732
  20.6 19.4 %copy-start.6 = (f32[4,3,1024]{2,0,1:T(4,128)S(1)}, f32[4,3,1024]{2,0,1:T(4,128)}, u32[]{:S(2)}) copy-start(f32[4,3,1024]{2,0,1:T(4,128)} %param.13) | copy-start | bytes 147460
  20.6 42.4 %collective-permute-start.1 = (bf16[2,32,1024]{2,1,0:T(8,128)(2,1)}, bf16[2,32,1024]{2,1,0:T(8,128)(2,1)S(1)}, u32[]{:S(2)}, u32[]{:S(2)}) collective-permute-start(bf16[2,32,1024]{2,1,0:T(8,128)(2,1)} %slice.597), channel_id=1, source_target_pairs={{1,0},{2,1},{3,2},{4,3},{5,4},{6,5},{7,6},{8,7},{9,8},{10,9},{11,1... | collective-permute-start | bytes 393224 | tf_op jit(solution)/shard_map/ppermute | solution.py:21
  25.2 37.7 %all-to-all-start = ((f32[4,2,32,256]{3,2,1,0:T(8,128)}), f32[4,2,32,256]{3,2,1,0:T(8,128)S(1)}, u32[]{:S(2)}, u32[]{:S(2)}) async-start(f32[4,2,32,256]{3,2,1,0:T(8,128)} %broadcast_in_dim.78), calls=%async_computation | async-start | bytes 524288 | tf_op jit(solution)/shard_map/all_to_all | solution.py:46
  57.3 3.9 %copy-start.4 = (bf16[1024,1024]{1,0:T(8,128)(2,1)S(1)}, bf16[1024,1024]{1,0:T(8,128)(2,1)}, u32[]{:S(2)}) copy-start(bf16[1024,1024]{1,0:T(8,128)(2,1)} %get-tuple-element.155) | copy-start | bytes 6291460
  63.0 1.0 copy-start.19
  64.0 22.0 %all-to-all-start.1 = ((f32[4,5,32,256]{3,2,1,0:T(8,128)}), f32[4,5,32,256]{3,2,1,0:T(8,128)S(1)}, u32[]{:S(2)}, u32[]{:S(2)}) async-start(f32[4,5,32,256]{3,2,1,0:T(8,128)} %broadcast_in_dim.80), calls=%async_computation.1 | async-start | bytes 1310720 | tf_op jit(solution)/shard_map/all_to_all | solution.py:46
  79.7 2.3 %copy-start.12 = (f32[32,1024]{1,0:T(8,128)S(1)}, f32[32,1024]{1,0:T(8,128)}, u32[]{:S(2)}) copy-start(f32[32,1024]{1,0:T(8,128)} %convolution_multiply_fusion.9) | copy-start | bytes 393220
  79.7 2.3 %copy-start.20 = (bf16[2,32,1024]{2,1,0:T(8,128)(2,1)S(1)}, bf16[2,32,1024]{2,1,0:T(8,128)(2,1)}, u32[]{:S(2)}) copy-start(bf16[2,32,1024]{2,1,0:T(8,128)(2,1)} %copy-done.19) | copy-start | bytes 393220
  87.3 28.5 %all-to-all-start.2 = ((f32[4,9,32,256]{3,2,1,0:T(8,128)}), f32[4,9,32,256]{3,2,1,0:T(8,128)}, u32[]{:S(2)}, u32[]{:S(2)}) async-start(f32[4,9,32,256]{3,2,1,0:T(8,128)} %broadcast_in_dim.82), calls=%async_computation.2 | async-start | bytes 2359296 | tf_op jit(solution)/shard_map/all_to_all | solution.py:46
  102.5 0.9 copy-start.8
  102.6 1.0 copy-start.9
  102.6 4.9 %copy-start.10 = (f32[32,1024]{1,0:T(8,128)S(1)}, f32[32,1024]{1,0:T(8,128)}, u32[]{:S(2)}) copy-start(f32[32,1024]{1,0:T(8,128)} %convolution_multiply_fusion.16) | copy-start | bytes 393220
  103.5 5.9 %copy-start.11 = (f32[32,1024]{1,0:T(8,128)S(1)}, f32[32,1024]{1,0:T(8,128)}, u32[]{:S(2)}) copy-start(f32[32,1024]{1,0:T(8,128)} %convolution_multiply_fusion.13) | copy-start | bytes 393220
  104.3 40.6 %collective-permute-start.2 = (f32[3,32,1024]{2,1,0:T(8,128)}, f32[3,32,1024]{2,1,0:T(8,128)}, u32[]{:S(2)}, u32[]{:S(2)}) collective-permute-start(f32[3,32,1024]{2,1,0:T(8,128)} %pad_maximum_fusion.1), channel_id=1, source_target_pairs={{0,1},{1,2},{2,3},{3,4},{4,5},{5,6},{6,7},{7,8},{8,9},{9,10},{10,1... | collective-permute-start | bytes 1179656 | tf_op jit(solution)/shard_map/ppermute | solution.py:181
  110.6 1.5 copy-start.16
  110.7 3.2 %copy-start.15 = (f32[32,1024]{1,0:T(8,128)S(1)}, f32[32,1024]{1,0:T(8,128)}, u32[]{:S(2)}) copy-start(f32[32,1024]{1,0:T(8,128)} %fusion.12) | copy-start | bytes 393220
  110.7 3.2 %copy-start.21 = (bf16[2,32,1024]{2,1,0:T(8,128)(2,1)S(1)}, bf16[2,32,1024]{2,1,0:T(8,128)(2,1)}, u32[]{:S(2)}) copy-start(bf16[2,32,1024]{2,1,0:T(8,128)(2,1)} %copy-done.19) | copy-start | bytes 393220
  112.1 4.6 %copy-start.7 = (f32[4,3,1024]{2,0,1:T(4,128)S(1)}, f32[4,3,1024]{2,0,1:T(4,128)}, u32[]{:S(2)}) copy-start(f32[4,3,1024]{2,0,1:T(4,128)} %param.13) | copy-start | bytes 147460
  117.4 35.8 %all-to-all-start.3 = ((bf16[8,32,256]{2,1,0:T(8,128)(2,1)}), bf16[8,32,256]{2,1,0:T(8,128)(2,1)S(1)}, u32[]{:S(2)}, u32[]{:S(2)}) async-start(bf16[8,32,256]{2,1,0:T(8,128)(2,1)} %broadcast_in_dim.83), calls=%async_computation.3 | async-start | bytes 262144 | tf_op jit(solution)/shard_map/all_to_all | solution.py:46
  133.6 5.0 %copy-start.18 = (f32[32,1024]{1,0:T(8,128)S(1)}, f32[32,1024]{1,0:T(8,128)}, u32[]{:S(2)}) copy-start(f32[32,1024]{1,0:T(8,128)} %fusion.16) | copy-start | bytes 393220
  137.8 4.1 %copy-start.2 = (bf16[1024,1024]{1,0:T(8,128)(2,1)S(1)}, bf16[1024,1024]{1,0:T(8,128)(2,1)}, u32[]{:S(2)}) copy-start(bf16[1024,1024]{1,0:T(8,128)(2,1)} %get-tuple-element.112) | copy-start | bytes 6291460
  138.7 4.9 %copy-start.3 = (bf16[1024,1024]{1,0:T(8,128)(2,1)S(1)}, bf16[1024,1024]{1,0:T(8,128)(2,1)}, u32[]{:S(2)}) copy-start(bf16[1024,1024]{1,0:T(8,128)(2,1)} %get-tuple-element.113) | copy-start | bytes 6291460
  138.7 4.9 %copy-start.17 = (f32[32,1024]{1,0:T(8,128)S(1)}, f32[32,1024]{1,0:T(8,128)}, u32[]{:S(2)}) copy-start(f32[32,1024]{1,0:T(8,128)} %fusion.11) | copy-start | bytes 393220
  141.8 3.1 %copy-start.14 = (f32[32,1024]{1,0:T(8,128)S(1)}, f32[32,1024]{1,0:T(8,128)}, u32[]{:S(2)}) copy-start(f32[32,1024]{1,0:T(8,128)} %fusion.22) | copy-start | bytes 393220
  143.6 5.6 %copy-start.1 = (bf16[1024,1024]{1,0:T(8,128)(2,1)S(1)}, bf16[1024,1024]{1,0:T(8,128)(2,1)}, u32[]{:S(2)}) copy-start(bf16[1024,1024]{1,0:T(8,128)(2,1)} %get-tuple-element.114) | copy-start | bytes 6291460
  157.4 2.3 %copy-start.13 = (f32[1,32,1024]{2,1,0:T(8,128)S(1)}, f32[1,32,1024]{2,1,0:T(8,128)}, u32[]{:S(2)}) copy-start(f32[1,32,1024]{2,1,0:T(8,128)} %fusion.59) | copy-start | bytes 393220
  159.7 1.6 copy-start.26
where the time goes:
time: 168 us; the launch traced here: 166 us
  matrix products  55.1 us (33%)
  other arithmetic  48.5 us (29%)
  starting transfers between devices  38.2 us (23%)
  local copies, waits for them, and re-layouts  18.3 us (11%)
  between operations  6.08 us (4%)
    convert_element_type x6, other arithmetic, matern(): return (amplitude * (1.0 + scaled) * jnp.exp(-scaled)).astype(jnp.bfloat16)  42.3 us
    dot_general x8, matrix products, run_job(): lax.dot_general(values[b], tile, (((1,), (1,)), ((), ())), preferred_elem...  19.5 us
    ppermute x2, starting transfers between devices, with_halo(): return lax.ppermute(leading, axis, [(b, a) for a, b in up])  18 us
    all_to_all x4, starting transfers between devices, from_everyone(): lax.all_to_all(jnp.broadcast_to(value[None], (peers, *value.shape)), axis...  17.1 us
    dot_general x4, matrix products, run_job(): jnp.dot(values[b], tile, preferred_element_type=f32)  9.65 us
    dot_general x5, matrix products, run_job(): jnp.dot(values[a], tile, preferred_element_type=f32)  6.4 us
    dot_general x1, matrix products, on_device(): lax.dot_general(result, hots, (((2,), (2,)), ((0,), (0,))), preferred_ele...  4.88 us
    slice x6, local copies, waits for them, and re-layouts, matern(): square = (source[0][:, None] - target[0][None, :]) ** 2  3.96 us
  transfers between devices with their start and end apart: 7, of which 0 were waited for; matrix products, arithmetic and copies ran while one was open for 63% of the time, Pallas kernels for 0%

commit v1 on v0

--- a/solution.py
+++ b/solution.py
@@ -122,9 +122,9 @@
         tile = lax.optimization_barrier(matern(at[a], at[b], signal_variance))
         if a == b:
             t = b - NEAR_REACH
-            near[t] = near[t] + jnp.dot(values[b], tile, preferred_element_type=f32) * pattern[
-                t, NEAR_REACH
-            ]
+            near[t] = near[t] + lax.dot_general(
+                values[b], tile, (((1,), (1,)), ((), ())), preferred_element_type=f32
+            ) * pattern[t, NEAR_REACH]
             return
         gap = b - a
         if b in own:

time: 168 us -> 169 us (level)
    dot_general x8 -> x12, matrix products: 19.5 us -> 30.2 us  [run_job(): lax.dot_general(values[b], tile, (((1,), (1,)), ((), ())), preferred_elem...]
    dot_general x4 -> x0, matrix products: 9.65 us -> none  [run_job(): jnp.dot(values[b], tile, preferred_element_type=f32)]
  transfers between devices with their start and end apart: 7 -> 7, of which waited for: 0 -> 0; matrix products, arithmetic and copies ran while one was open for 63% -> 64% of each run, Pallas kernels for 0% -> 0%
where the time goes in v1:
time: 169 us; the launch traced here: 167 us
  matrix products  56.1 us (33%)
  other arithmetic  48.5 us (29%)
  starting transfers between devices  38.2 us (23%)
  local copies, waits for them, and re-layouts  18.3 us (11%)
  between operations  6.08 us (4%)
    convert_element_type x6, other arithmetic, matern(): return (amplitude * (1.0 + scaled) * jnp.exp(-scaled)).astype(jnp.bfloat16)  42.3 us
    dot_general x12, matrix products, run_job(): lax.dot_general(values[b], tile, (((1,), (1,)), ((), ())), preferred_elem...  30.2 us
    ppermute x2, starting transfers between devices, with_halo(): return lax.ppermute(leading, axis, [(b, a) for a, b in up])  18 us
    all_to_all x4, starting transfers between devices, from_everyone(): lax.all_to_all(jnp.broadcast_to(value[None], (peers, *value.shape)), axis...  17.1 us
    dot_general x5, matrix products, run_job(): jnp.dot(values[a], tile, preferred_element_type=f32)  6.4 us
    dot_general x1, matrix products, on_device(): lax.dot_general(result, hots, (((2,), (2,)), ((0,), (0,))), preferred_ele...  4.88 us
    slice x6, local copies, waits for them, and re-layouts, matern(): square = (source[0][:, None] - target[0][None, :]) ** 2  3.96 us
    dot_general x1, matrix products, on_device(): lax.dot_general(probes, hots, (((2,), (1,)), ((0,), (0,))), preferred_ele...  3.94 us
  transfers between devices with their start and end apart: 7, of which 0 were waited for; matrix products, arithmetic and copies ran while one was open for 64% of the time, Pallas kernels for 0%

profile of v1, /device:TPU:1, one launch (start us, length us, event | category | flops | bytes accessed | tf_op | source)
XLA Modules:
  0.0 167.2 jit_solution(7047589010350608474)
XLA Ops:
  0.0 1.0 slice.482
  1.0 15.0 %collective-permute-start = (f32[2,3,1024]{2,0,1:T(2,128)S(1)}, f32[2,3,1024]{2,0,1:T(2,128)}, u32[]{:S(2)}, u32[]{:S(2)}) collective-permute-start(f32[2,3,1024]{2,0,1:T(2,128)S(1)} %slice.482), channel_id=1, source_target_pairs={{1,0},{2,1},{3,2},{4,3},{5,4},{6,5},{7,6},{8,7},{9,8},{10,9},{11,1... | collective-permute-start | bytes 73736 | tf_op jit(solution)/shard_map/ppermute | solution.py:21
  15.9 3.9 %fusion.6 = bf16[4,1024,32]{1,2,0:T(8,128)(2,1)S(1)} fusion(bf16[4,32,1024]{2,1,0:T(8,128)(2,1)} %param.12, s32[4,1024]{1,0:T(4,128)} %param.14), kind=kOutput, calls=%fused_computation.24 | convolution fusion | flops 272760832 | bytes 540672 | tf_op jit(solution)/shard_map/dot_general | solution.py:88
  19.9 0.7 slice.597
  20.6 3.0 %collective-permute-start.1 = (bf16[2,32,1024]{2,1,0:T(8,128)(2,1)}, bf16[2,32,1024]{2,1,0:T(8,128)(2,1)S(1)}, u32[]{:S(2)}, u32[]{:S(2)}) collective-permute-start(bf16[2,32,1024]{2,1,0:T(8,128)(2,1)} %slice.597), channel_id=1, source_target_pairs={{1,0},{2,1},{3,2},{4,3},{5,4},{6,5},{7,6},{8,7},{9,8},{10,9},{11,1... | collective-permute-start | bytes 393224 | tf_op jit(solution)/shard_map/ppermute | solution.py:21
  24.5 0.7 broadcast_in_dim.78
  25.2 3.4 %all-to-all-start = ((f32[4,2,32,256]{3,2,1,0:T(8,128)}), f32[4,2,32,256]{3,2,1,0:T(8,128)S(1)}, u32[]{:S(2)}, u32[]{:S(2)}) async-start(f32[4,2,32,256]{3,2,1,0:T(8,128)} %broadcast_in_dim.78), calls=%async_computation | async-start | bytes 524288 | tf_op jit(solution)/shard_map/all_to_all | solution.py:46
  28.8 0.6 iota_compare_fusion.7
  29.4 0.7 slice.514
  30.0 0.7 fusion.123
  32.3 0.7 fusion.124
  36.9 0.6 pad_clamp_fusion
  37.5 1.1 constant_dynamic-slice_fusion.5
  38.7 0.6 slice_reduce_fusion.5
  39.3 0.6 copy.32
  40.0 4.3 %multiply_convert_fusion.11 = bf16[1024,1024]{1,0:T(8,128)(2,1)} fusion(f32[1024]{0:T(1024)S(1)} %bitcast.362, f32[1024]{0:T(1024)S(1)} %bitcast.363, f32[1024]{0:T(1024)S(1)} %bitcast.361, f32[]{:T(128)S(6)} %copy.46), kind=kLoop, calls=%fused_computation.17 | loop fusion | flops 14680064 | bytes 2109444 | tf_op jit(solution)/shard_map/convert_element_type | solution.py:61
  44.2 7.6 %multiply_convert_fusion.2 = (bf16[1024,1024]{1,0:T(8,128)(2,1)}, bf16[1024,1024]{1,0:T(8,128)(2,1)}) fusion(f32[1024]{0:T(1024)S(1)} %bitcast.346, f32[1024]{0:T(1024)S(1)} %bitcast.347, f32[1024]{0:T(1024)S(1)} %bitcast.348, f32[]{:T(128)S(6)} %copy.46, f32[1024]{0:T(1024)S(1)} %bitcast.349, f32[1024]{0:T(1024)S(1)} %bitcast.350, f32[1024]{0:T(1024)S(1)} %bitcast.351), kind=kLoop, calls=%fused_computation.8 | loop fusion | flops 29360128 | bytes 4218884 | tf_op jit(solution)/shard_map/convert_element_type | solution.py:61
  51.8 3.7 %convolution_multiply_fusion.16 = f32[32,1024]{1,0:T(8,128)} fusion(bf16[1024,1024]{1,0:T(8,128)(2,1)} %multiply_convert_fusion.11, f32[]{:T(128)} %bitcast.55, bf16[4,32,1024]{2,1,0:T(8,128)(2,1)S(1)} %bitcast.289), kind=kOutput, calls=%fused_computation.60 | convolution fusion | flops 67141632 | bytes 2293764 | tf_op jit(solution)/shard_map/dot_general | solution.py:125
  55.5 1.3 constant_dynamic-slice_fusion.1
  56.9 0.7 stack.89
  57.6 0.5 compare_and_fusion
  58.1 3.6 %convolution_multiply_fusion.9 = f32[32,1024]{1,0:T(8,128)} fusion(bf16[1024,1024]{1,0:T(8,128)(2,1)} %get-tuple-element.154, f32[]{:T(128)} %bitcast.125, bf16[4,32,1024]{2,1,0:T(8,128)(2,1)S(1)} %bitcast.290), kind=kOutput, calls=%fused_computation.48 | convolution fusion | flops 67141632 | bytes 2293764 | tf_op jit(solution)/shard_map/dot_general | solution.py:125
  61.8 2.0 %convolution_multiply_fusion.13 = f32[32,1024]{1,0:T(8,128)} fusion(bf16[1024,1024]{1,0:T(8,128)(2,1)S(1)} %copy-done.4, f32[]{:T(128)} %bitcast.102, bf16[4,32,1024]{2,1,0:T(8,128)(2,1)S(1)} %bitcast.291), kind=kOutput, calls=%fused_computation.55 | convolution fusion | flops 67141632 | bytes 2293764 | tf_op jit(solution)/shard_map/dot_general | solution.py:125
  63.8 0.9 broadcast_in_dim.80
  64.8 3.7 %all-to-all-start.1 = ((f32[4,5,32,256]{3,2,1,0:T(8,128)}), f32[4,5,32,256]{3,2,1,0:T(8,128)S(1)}, u32[]{:S(2)}, u32[]{:S(2)}) async-start(f32[4,5,32,256]{3,2,1,0:T(8,128)} %broadcast_in_dim.80), calls=%async_computation.1 | async-start | bytes 1310720 | tf_op jit(solution)/shard_map/all_to_all | solution.py:46
  68.4 0.9 fusion.120
  69.3 10.0 %multiply_convert_fusion.7 = (bf16[1024,1024]{1,0:T(8,128)(2,1)S(1)}, bf16[1024,1024]{1,0:T(8,128)(2,1)S(1)}, bf16[1024,1024]{1,0:T(8,128)(2,1)S(1)}) fusion(f32[1024]{0:T(1024)S(1)} %bitcast.353, f32[1024]{0:T(1024)S(1)} %bitcast.354, f32[1024]{0:T(1024)S(1)} %bitcast.352, f32[1024]{0:T(1024)S(1)} %bitcast.359, f32[1024]{0:T(1024)S(1)} %bitcast.358, ...), kind=kLoop, calls=%fused_computation.13 | loop fusion | flops 44040192 | bytes 6328324 | tf_op jit(solution)/shard_map/convert_element_type | solution.py:61
  79.4 1.1 convolution_bitcast_fusion.1
  80.5 1.1 convolution_bitcast_fusion.2
  81.6 1.4 convolution_multiply_fusion.4
  83.1 2.0 %fusion.17 = f32[32,1024]{1,0:T(8,128)} fusion(f32[32,1024]{1,0:T(8,128)S(1)} %copy-done.12, bf16[1024,1024]{1,0:T(8,128)(2,1)S(1)} %get-tuple-element.115, f32[]{:T(128)} %bitcast.127, bf16[2,32,1024]{2,1,0:T(8,128)(2,1)S(1)} %copy-done.20), kind=kOutput, calls=%fused_computation.47 | convolution fusion | flops 67174400 | bytes 2424836 | tf_op jit(solution)/shard_map/dot_general | solution.py:137
  85.1 1.9 %fusion.12 = f32[32,1024]{1,0:T(8,128)} fusion(f32[32,1024]{1,0:T(8,128)S(1)} %convolution_multiply_fusion.4, bf16[1024,1024]{1,0:T(8,128)(2,1)S(1)} %get-tuple-element.116, f32[]{:T(128)} %bitcast.134, bf16[2,32,1024]{2,1,0:T(8,128)(2,1)S(1)} %copy-done.20), kind=kOutput, calls=%fused_computation.37 | convolution fusion | flops 67174400 | bytes 2424836 | tf_op jit(solution)/shard_map/dot_general | solution.py:137
  87.2 1.2 broadcast_in_dim.82
  88.3 4.3 %all-to-all-start.2 = ((f32[4,9,32,256]{3,2,1,0:T(8,128)}), f32[4,9,32,256]{3,2,1,0:T(8,128)}, u32[]{:S(2)}, u32[]{:S(2)}) async-start(f32[4,9,32,256]{3,2,1,0:T(8,128)} %broadcast_in_dim.82), calls=%async_computation.2 | async-start | bytes 2359296 | tf_op jit(solution)/shard_map/all_to_all | solution.py:46
  92.6 1.0 fusion.118
  93.6 3.3 %multiply_convert_fusion.6 = bf16[1024,1024]{1,0:T(8,128)(2,1)S(1)} fusion(f32[1024]{0:T(1024)S(1)} %bitcast.344, f32[1024]{0:T(1024)S(1)} %bitcast.340, f32[1024]{0:T(1024)S(1)} %bitcast.343, f32[1024]{0:T(1024)S(1)} %bitcast.341, f32[1024]{0:T(1024)S(1)} %bitcast.345, f32[1024]{0:T(1024)S(1)} %bitcast.342, f32[]{:T(128)S(6)} %copy.46), kind=kLoop, calls=%fused_computation.12 | loop fusion | flops 14680064 | bytes 2121732 | tf_op jit(solution)/shard_map/convert_element_type | solution.py:61
  96.9 6.7 %multiply_convert_fusion.10 = (bf16[1024,1024]{1,0:T(8,128)(2,1)S(1)}, bf16[1024,1024]{1,0:T(8,128)(2,1)S(1)}) fusion(f32[1024]{0:T(1024)S(1)} %bitcast.335, f32[1024]{0:T(1024)S(1)} %bitcast.336, f32[1024]{0:T(1024)S(1)} %bitcast.337, f32[1024]{0:T(1024)S(1)} %bitcast.338, f32[1024]{0:T(1024)S(1)} %bitcast.339, f32[1024]{0:T(1024)S(1)} %bitcast.331, ...), kind=kLoop, calls=%fused_computation.16 | loop fusion | flops 29360128 | bytes 4231172 | tf_op jit(solution)/shard_map/convert_element_type | solution.py:61
  104.6 0.8 pad_maximum_fusion.1
  105.4 3.1 %collective-permute-start.2 = (f32[3,32,1024]{2,1,0:T(8,128)}, f32[3,32,1024]{2,1,0:T(8,128)}, u32[]{:S(2)}, u32[]{:S(2)}) collective-permute-start(f32[3,32,1024]{2,1,0:T(8,128)} %pad_maximum_fusion.1), channel_id=1, source_target_pairs={{0,1},{1,2},{2,3},{3,4},{4,5},{5,6},{6,7},{7,8},{8,9},{9,10},{10,1... | collective-permute-start | bytes 1179656 | tf_op jit(solution)/shard_map/ppermute | solution.py:181
  108.5 1.9 %fusion.22 = f32[32,1024]{1,0:T(8,128)} fusion(f32[32,1024]{1,0:T(8,128)S(1)} %copy-done.10, bf16[1024,1024]{1,0:T(8,128)(2,1)S(1)} %get-tuple-element.110, f32[]{:T(128)} %bitcast.63, bf16[4,32,1024]{2,1,0:T(8,128)(2,1)S(1)} %bitcast.296), kind=kOutput, calls=%fused_computation.59 | convolution fusion | flops 67174400 | bytes 2424836 | tf_op jit(solution)/shard_map/dot_general | solution.py:137
  110.5 1.2 fusion.20
  111.8 1.4 fusion.19
  113.2 1.7 %fusion.16 = f32[32,1024]{1,0:T(8,128)} fusion(f32[32,1024]{1,0:T(8,128)S(1)} %copy-done.16, bf16[1024,1024]{1,0:T(8,128)(2,1)S(1)} %get-tuple-element.111, f32[]{:T(128)} %bitcast.128, bf16[4,32,1024]{2,1,0:T(8,128)(2,1)S(1)} %bitcast.299), kind=kOutput, calls=%fused_computation.45 | convolution fusion | flops 67174400 | bytes 2424836 | tf_op jit(solution)/shard_map/dot_general | solution.py:132
  114.9 1.9 %fusion.11 = f32[32,1024]{1,0:T(8,128)} fusion(f32[32,1024]{1,0:T(8,128)S(1)} %copy-done.15, bf16[1024,1024]{1,0:T(8,128)(2,1)S(1)} %multiply_convert_fusion.6, f32[]{:T(128)} %bitcast.136, bf16[2,32,1024]{2,1,0:T(8,128)(2,1)S(1)} %copy-done.21), kind=kOutput, calls=%fused_computation.35 | convolution fusion | flops 67174400 | bytes 2424836 | tf_op jit(solution)/shard_map/dot_general | solution.py:137
  116.8 0.9 slice_reduce_fusion
  117.8 0.7 broadcast_in_dim.83
  118.5 5.7 %all-to-all-start.3 = ((bf16[8,32,256]{2,1,0:T(8,128)(2,1)}), bf16[8,32,256]{2,1,0:T(8,128)(2,1)S(1)}, u32[]{:S(2)}, u32[]{:S(2)}) async-start(bf16[8,32,256]{2,1,0:T(8,128)(2,1)} %broadcast_in_dim.83), calls=%async_computation.3 | async-start | bytes 262144 | tf_op jit(solution)/shard_map/all_to_all | solution.py:46
  124.2 10.5 %multiply_convert_fusion.9 = (bf16[1024,1024]{1,0:T(8,128)(2,1)}, bf16[1024,1024]{1,0:T(8,128)(2,1)}, bf16[1024,1024]{1,0:T(8,128)(2,1)}) fusion(f32[1024]{0:T(1024)S(1)} %bitcast.326, f32[1024]{0:T(1024)S(1)} %bitcast.327, f32[1024]{0:T(1024)S(1)} %bitcast.328, f32[1024]{0:T(1024)S(1)} %bitcast.329, f32[1024]{0:T(1024)S(1)} %bitcast.330, ...), kind=kLoop, calls=%fused_computation.15 | loop fusion | flops 44040192 | bytes 6340612 | tf_op jit(solution)/shard_map/convert_element_type | solution.py:61
  134.7 1.3 slice.606
  136.0 1.0 pad_maximum_fusion
  137.0 1.8 %gather_fusion = bf16[6,32,256]{2,1,0:T(8,128)(2,1)S(1)} fusion(bf16[48,32,256]{2,1,0:T(8,128)(2,1)} %pad_maximum_fusion, s32[1024]{0:T(1024)} %pad_clamp_fusion), kind=kCustom, calls=%fused_computation | custom fusion | bytes 196632 | tf_op jit(solution)/shard_map/jit(_take)/gather | solution.py:225
  138.8 0.9 fusion.65
  139.7 3.1 %fusion.15 = f32[32,1024]{1,0:T(8,128)S(1)} fusion(f32[32,1024]{1,0:T(8,128)S(1)} %copy-done.18, bf16[1024,1024]{1,0:T(8,128)(2,1)} %get-tuple-element.113, f32[]{:T(128)} %bitcast.129, bf16[4,32,1024]{2,1,0:T(8,128)(2,1)S(1)} %bitcast.300), kind=kOutput, calls=%fused_computation.43 | convolution fusion | flops 67174400 | bytes 2424836 | tf_op jit(solution)/shard_map/dot_general | solution.py:137
  142.9 1.1 fusion.14
  144.0 0.6 copy.30
  144.6 1.3 fusion.10
  146.0 4.2 %fusion.59 = f32[1,32,1024]{2,1,0:T(8,128)} fusion(f32[3,32,1024]{2,1,0:T(8,128)} %collective-permute-done.2, f32[32,1024]{1,0:T(8,128)S(1)} %copy-done.14, bf16[1024,1024]{1,0:T(8,128)(2,1)S(1)} %copy-done.2, f32[]{:T(128)} %bitcast.95, f32[]{:T(128)} %bitcast.93, f32[]{:T(128)} %bitcast.71, bf16[4,32,1024]{2,1,0:T(8,128)(2,1)S(1)} %bitcast.303), kind=kOutput, calls=%fused_computation.100 | convolution fusion | flops 67305472 | bytes 2686988 | tf_op jit(solution)/shard_map/dot_general | solution.py:137
  150.2 2.9 %fusion.56 = f32[1,32,1024]{2,1,0:T(8,128)S(1)} fusion(f32[3,32,1024]{2,1,0:T(8,128)} %collective-permute-done.2, f32[32,1024]{1,0:T(8,128)S(1)} %fusion.19, bf16[1024,1024]{1,0:T(8,128)(2,1)S(1)} %copy-done.1, f32[]{:T(128)} %bitcast.118, f32[]{:T(128)} %bitcast.117, bf16[4,32,1024]{2,1,0:T(8,128)(2,1)S(1)} %bitcast.304), kind=kOutput, calls=%fused_computation.96 | convolution fusion | flops 67239936 | bytes 2555912 | tf_op jit(solution)/shard_map/dot_general | solution.py:137
  153.1 1.1 fusion.9
  154.3 0.8 select_bitcast_fusion
  155.0 3.4 %fusion.26 = f32[32,256]{1,0:T(8,128)} fusion(bf16[32,2048]{1,0:T(8,128)(2,1)S(1)} %bitcast.311, f32[256]{0:T(256)} %bitcast.367, f32[2048]{0:T(1024)S(1)} %bitcast.317, f32[256]{0:T(256)} %bitcast.368, f32[2048]{0:T(1024)} %bitcast.318, f32[256]{0:T(256)} %bitcast.369, f32[2048]{0:T(1024)S(1)} %bitcast.316, f32[]{:T(128)S(6)} %copy.46, ...), kind=kOutput, calls=%fused_computation.69 | convolution fusion | flops 45096960 | bytes 322564 | tf_op jit(solution)/shard_map/dot_general | solution.py:231
  158.4 2.3 %fusion.27 = bf16[32,256,1]{1,0,2:T(8,128)(2,1)S(1)} fusion(f32[32,256]{1,0:T(8,128)} %fusion.26, bf16[32,1536]{1,0:T(8,128)(2,1)} %bitcast.314, f32[256]{0:T(256)} %bitcast.366, f32[1536]{0:T(1024)} %get-tuple-element.44, f32[256]{0:T(256)} %bitcast.365, f32[1536]{0:T(1024)} %get-tuple-element.45, f32[256]{0:T(256)} %bitcast.364, ...), kind=kOutput, calls=%fused_computation.70 | convolution fusion | flops 30687232 | bytes 168964 | tf_op jit(solution)/shard_map/dot_general | solution.py:229
  160.8 1.6 fusion.5
  162.3 4.9 %fusion.7 = bf16[4,32,1024]{2,1,0:T(8,128)(2,1)} fusion(bf16[4,32,1024]{2,1,0:T(8,128)(2,1)} %fusion.5, s32[4,1024]{1,0:T(4,128)S(1)} %copy-done.26), kind=kOutput, calls=%fused_computation.25 | convolution fusion | flops 272760832 | bytes 540672 | tf_op jit(solution)/shard_map/dot_general | solution.py:245
  (92 shorter events, 2.4 us)
Async XLA Ops:
  0.0 23.7 %copy-start = (bf16[4,1024,256]{2,1,0:T(8,128)(2,1)S(1)}, bf16[4,1024,256]{2,1,0:T(8,128)(2,1)}, u32[]{:S(2)}) copy-start(bf16[4,1024,256]{2,1,0:T(8,128)(2,1)} %param.15) | copy-start | bytes 6291460
  1.0 62.8 %collective-permute-start = (f32[2,3,1024]{2,0,1:T(2,128)S(1)}, f32[2,3,1024]{2,0,1:T(2,128)}, u32[]{:S(2)}, u32[]{:S(2)}) collective-permute-start(f32[2,3,1024]{2,0,1:T(2,128)S(1)} %slice.482), channel_id=1, source_target_pairs={{1,0},{2,1},{3,2},{4,3},{5,4},{6,5},{7,6},{8,7},{9,8},{10,9},{11,1... | collective-permute-start | bytes 73736 | tf_op jit(solution)/shard_map/ppermute | solution.py:21
  19.9 4.3 %copy-start.5 = (bf16[1,4,256,256]{3,2,1,0:T(8,128)(2,1)S(1)}, bf16[1,4,256,256]{3,2,1,0:T(8,128)(2,1)}, u32[]{:S(2)}) copy-start(bf16[1,4,256,256]{3,2,1,0:T(8,128)(2,1)} %param.16) | copy-start | bytes 1572868
  19.9 4.4 %copy-start.22 = (bf16[1,256,256]{2,1,0:T(8,128)(2,1)S(1)}, bf16[1,256,256]{2,1,0:T(8,128)(2,1)}, u32[]{:S(2)}) copy-start(bf16[1,256,256]{2,1,0:T(8,128)(2,1)} %param.17) | copy-start | bytes 393220
  20.6 8.8 %copy-start.25 = (s32[4,5]{1,0:T(4,128)S(1)}, s32[4,5]{1,0:T(4,128)}, u32[]{:S(2)}) copy-start(s32[4,5]{1,0:T(4,128)} %param.20) | copy-start | bytes 244
  20.6 11.7 %copy-start.24 = (s32[1,9]{1,0:T(1,128)S(1)}, s32[1,9]{1,0:T(1,128)}, u32[]{:S(2)}) copy-start(s32[1,9]{1,0:T(1,128)} %param.21) | copy-start | bytes 112
  20.6 18.7 %copy-start.23 = (f32[8,3,256]{2,0,1:T(8,128)S(1)}, f32[8,3,256]{2,0,1:T(8,128)}, u32[]{:S(2)}) copy-start(f32[8,3,256]{2,0,1:T(8,128)} %param.19) | copy-start | bytes 73732
  20.6 19.4 %copy-start.6 = (f32[4,3,1024]{2,0,1:T(4,128)S(1)}, f32[4,3,1024]{2,0,1:T(4,128)}, u32[]{:S(2)}) copy-start(f32[4,3,1024]{2,0,1:T(4,128)} %param.13) | copy-start | bytes 147460
  20.6 43.2 %collective-permute-start.1 = (bf16[2,32,1024]{2,1,0:T(8,128)(2,1)}, bf16[2,32,1024]{2,1,0:T(8,128)(2,1)S(1)}, u32[]{:S(2)}, u32[]{:S(2)}) collective-permute-start(bf16[2,32,1024]{2,1,0:T(8,128)(2,1)} %slice.597), channel_id=1, source_target_pairs={{1,0},{2,1},{3,2},{4,3},{5,4},{6,5},{7,6},{8,7},{9,8},{10,9},{11,1... | collective-permute-start | bytes 393224 | tf_op jit(solution)/shard_map/ppermute | solution.py:21
  25.2 38.5 %all-to-all-start = ((f32[4,2,32,256]{3,2,1,0:T(8,128)}), f32[4,2,32,256]{3,2,1,0:T(8,128)S(1)}, u32[]{:S(2)}, u32[]{:S(2)}) async-start(f32[4,2,32,256]{3,2,1,0:T(8,128)} %broadcast_in_dim.78), calls=%async_computation | async-start | bytes 524288 | tf_op jit(solution)/shard_map/all_to_all | solution.py:46
  57.6 4.2 %copy-start.4 = (bf16[1024,1024]{1,0:T(8,128)(2,1)S(1)}, bf16[1024,1024]{1,0:T(8,128)(2,1)}, u32[]{:S(2)}) copy-start(bf16[1024,1024]{1,0:T(8,128)(2,1)} %get-tuple-element.155) | copy-start | bytes 6291460
  63.8 1.0 copy-start.19
  64.8 22.2 %all-to-all-start.1 = ((f32[4,5,32,256]{3,2,1,0:T(8,128)}), f32[4,5,32,256]{3,2,1,0:T(8,128)S(1)}, u32[]{:S(2)}, u32[]{:S(2)}) async-start(f32[4,5,32,256]{3,2,1,0:T(8,128)} %broadcast_in_dim.80), calls=%async_computation.1 | async-start | bytes 1310720 | tf_op jit(solution)/shard_map/all_to_all | solution.py:46
  80.5 2.5 %copy-start.12 = (f32[32,1024]{1,0:T(8,128)S(1)}, f32[32,1024]{1,0:T(8,128)}, u32[]{:S(2)}) copy-start(f32[32,1024]{1,0:T(8,128)} %convolution_multiply_fusion.9) | copy-start | bytes 393220
  80.5 2.6 %copy-start.20 = (bf16[2,32,1024]{2,1,0:T(8,128)(2,1)S(1)}, bf16[2,32,1024]{2,1,0:T(8,128)(2,1)}, u32[]{:S(2)}) copy-start(bf16[2,32,1024]{2,1,0:T(8,128)(2,1)} %copy-done.19) | copy-start | bytes 393220
  88.3 28.5 %all-to-all-start.2 = ((f32[4,9,32,256]{3,2,1,0:T(8,128)}), f32[4,9,32,256]{3,2,1,0:T(8,128)}, u32[]{:S(2)}, u32[]{:S(2)}) async-start(f32[4,9,32,256]{3,2,1,0:T(8,128)} %broadcast_in_dim.82), calls=%async_computation.2 | async-start | bytes 2359296 | tf_op jit(solution)/shard_map/all_to_all | solution.py:46
  103.6 0.9 copy-start.8
  103.6 1.0 copy-start.9
  103.6 4.9 %copy-start.10 = (f32[32,1024]{1,0:T(8,128)S(1)}, f32[32,1024]{1,0:T(8,128)}, u32[]{:S(2)}) copy-start(f32[32,1024]{1,0:T(8,128)} %convolution_multiply_fusion.16) | copy-start | bytes 393220
  104.6 5.9 %copy-start.11 = (f32[32,1024]{1,0:T(8,128)S(1)}, f32[32,1024]{1,0:T(8,128)}, u32[]{:S(2)}) copy-start(f32[32,1024]{1,0:T(8,128)} %convolution_multiply_fusion.13) | copy-start | bytes 393220
  105.4 40.6 %collective-permute-start.2 = (f32[3,32,1024]{2,1,0:T(8,128)}, f32[3,32,1024]{2,1,0:T(8,128)}, u32[]{:S(2)}, u32[]{:S(2)}) collective-permute-start(f32[3,32,1024]{2,1,0:T(8,128)} %pad_maximum_fusion.1), channel_id=1, source_target_pairs={{0,1},{1,2},{2,3},{3,4},{4,5},{5,6},{6,7},{7,8},{8,9},{9,10},{10,1... | collective-permute-start | bytes 1179656 | tf_op jit(solution)/shard_map/ppermute | solution.py:181
  111.6 1.5 copy-start.16
  111.7 3.2 %copy-start.15 = (f32[32,1024]{1,0:T(8,128)S(1)}, f32[32,1024]{1,0:T(8,128)}, u32[]{:S(2)}) copy-start(f32[32,1024]{1,0:T(8,128)} %fusion.12) | copy-start | bytes 393220
  111.8 3.2 %copy-start.21 = (bf16[2,32,1024]{2,1,0:T(8,128)(2,1)S(1)}, bf16[2,32,1024]{2,1,0:T(8,128)(2,1)}, u32[]{:S(2)}) copy-start(bf16[2,32,1024]{2,1,0:T(8,128)(2,1)} %copy-done.19) | copy-start | bytes 393220
  113.2 4.6 %copy-start.7 = (f32[4,3,1024]{2,0,1:T(4,128)S(1)}, f32[4,3,1024]{2,0,1:T(4,128)}, u32[]{:S(2)}) copy-start(f32[4,3,1024]{2,0,1:T(4,128)} %param.13) | copy-start | bytes 147460
  118.5 35.8 %all-to-all-start.3 = ((bf16[8,32,256]{2,1,0:T(8,128)(2,1)}), bf16[8,32,256]{2,1,0:T(8,128)(2,1)S(1)}, u32[]{:S(2)}, u32[]{:S(2)}) async-start(bf16[8,32,256]{2,1,0:T(8,128)(2,1)} %broadcast_in_dim.83), calls=%async_computation.3 | async-start | bytes 262144 | tf_op jit(solution)/shard_map/all_to_all | solution.py:46
  134.7 5.0 %copy-start.18 = (f32[32,1024]{1,0:T(8,128)S(1)}, f32[32,1024]{1,0:T(8,128)}, u32[]{:S(2)}) copy-start(f32[32,1024]{1,0:T(8,128)} %fusion.16) | copy-start | bytes 393220
  138.8 4.1 %copy-start.2 = (bf16[1024,1024]{1,0:T(8,128)(2,1)S(1)}, bf16[1024,1024]{1,0:T(8,128)(2,1)}, u32[]{:S(2)}) copy-start(bf16[1024,1024]{1,0:T(8,128)(2,1)} %get-tuple-element.112) | copy-start | bytes 6291460
  139.7 4.9 %copy-start.3 = (bf16[1024,1024]{1,0:T(8,128)(2,1)S(1)}, bf16[1024,1024]{1,0:T(8,128)(2,1)}, u32[]{:S(2)}) copy-start(bf16[1024,1024]{1,0:T(8,128)(2,1)} %get-tuple-element.113) | copy-start | bytes 6291460
  139.7 4.9 %copy-start.17 = (f32[32,1024]{1,0:T(8,128)S(1)}, f32[32,1024]{1,0:T(8,128)}, u32[]{:S(2)}) copy-start(f32[32,1024]{1,0:T(8,128)} %fusion.11) | copy-start | bytes 393220
  142.9 3.1 %copy-start.14 = (f32[32,1024]{1,0:T(8,128)S(1)}, f32[32,1024]{1,0:T(8,128)}, u32[]{:S(2)}) copy-start(f32[32,1024]{1,0:T(8,128)} %fusion.22) | copy-start | bytes 393220
  144.6 5.6 %copy-start.1 = (bf16[1024,1024]{1,0:T(8,128)(2,1)S(1)}, bf16[1024,1024]{1,0:T(8,128)(2,1)}, u32[]{:S(2)}) copy-start(bf16[1024,1024]{1,0:T(8,128)(2,1)} %get-tuple-element.114) | copy-start | bytes 6291460
  158.4 2.3 %copy-start.13 = (f32[1,32,1024]{2,1,0:T(8,128)S(1)}, f32[1,32,1024]{2,1,0:T(8,128)}, u32[]{:S(2)}) copy-start(f32[1,32,1024]{2,1,0:T(8,128)} %fusion.59) | copy-start | bytes 393220
  160.7 1.6 copy-start.26

commit v2 on v0

--- a/solution.py
+++ b/solution.py
@@ -117,9 +117,8 @@
     near = [jnp.zeros((probe_count, leaf_size), f32) for _ in range(leaf_count)]
     outgoing = {}
 
-    def run_job(job, at, values):
+    def run_job(job, tile, values):
         a, b = job
-        tile = lax.optimization_barrier(matern(at[a], at[b], signal_variance))
         if a == b:
             t = b - NEAR_REACH
             near[t] = near[t] + jnp.dot(values[b], tile, preferred_element_type=f32) * pattern[
@@ -167,8 +166,11 @@
         else:
             own_coef = running.astype(jnp.bfloat16)
             group_coef = from_everyone(own_coef, "group")
-        for job in chunk:
-            run_job(job, at, values)
+        tiles = lax.optimization_barrier(
+            tuple(matern(at[a], at[b], signal_variance) for a, b in chunk)
+        )
+        for job, tile in zip(chunk, tiles):
+            run_job(job, tile, values)
         if step < len(rounds):
             running = jnp.sum(received[:, 0], axis=0)
             if step == 0:

time: 168 us -> 163 us (0.970)
  local copies, waits for them, and re-layouts: 18.3 us -> 16 us
  matrix products: 55.1 us -> 53.4 us
  transfers between devices with their start and end apart: 7 -> 7, of which waited for: 0 -> 0; matrix products, arithmetic and copies ran while one was open for 63% -> 62% of each run, Pallas kernels for 0% -> 0%
where the time goes in v2:
time: 163 us; the launch traced here: 162 us
  matrix products  53.4 us (33%)
  other arithmetic  47.7 us (29%)
  starting transfers between devices  38.5 us (24%)
  local copies, waits for them, and re-layouts  16 us (10%)
  between operations  6.12 us (4%)
    convert_element_type x6, other arithmetic, matern(): return (amplitude * (1.0 + scaled) * jnp.exp(-scaled)).astype(jnp.bfloat16)  43.3 us
    dot_general x8, matrix products, run_job(): lax.dot_general(values[b], tile, (((1,), (1,)), ((), ())), preferred_elem...  19.6 us
    ppermute x2, starting transfers between devices, with_halo(): return lax.ppermute(leading, axis, [(b, a) for a, b in up])  18 us
    all_to_all x4, starting transfers between devices, from_everyone(): lax.all_to_all(jnp.broadcast_to(value[None], (peers, *value.shape)), axis...  17.4 us
    dot_general x4, matrix products, run_job(): jnp.dot(values[b], tile, preferred_element_type=f32)  8.98 us
    dot_general x5, matrix products, run_job(): jnp.dot(values[a], tile, preferred_element_type=f32)  6.3 us
    dot_general x1, matrix products, on_device(): lax.dot_general(result, hots, (((2,), (2,)), ((0,), (0,))), preferred_ele...  4.88 us
    slice x6, local copies, waits for them, and re-layouts, matern(): square = (source[0][:, None] - target[0][None, :]) ** 2  4.71 us
  transfers between devices with their start and end apart: 7, of which 0 were waited for; matrix products, arithmetic and copies ran while one was open for 62% of the time, Pallas kernels for 0%

profile of v2, /device:TPU:1, one launch (start us, length us, event | category | flops | bytes accessed | tf_op | source)
XLA Modules:
  0.0 161.8 jit_solution(8194771391698735431)
XLA Ops:
  0.0 1.0 slice.482
  1.0 15.0 %collective-permute-start = (f32[2,3,1024]{2,0,1:T(2,128)S(1)}, f32[2,3,1024]{2,0,1:T(2,128)S(1)}, u32[]{:S(2)}, u32[]{:S(2)}) collective-permute-start(f32[2,3,1024]{2,0,1:T(2,128)S(1)} %slice.482), channel_id=1, source_target_pairs={{1,0},{2,1},{3,2},{4,3},{5,4},{6,5},{7,6},{8,7},{9,8},{10,9},{11,1... | collective-permute-start | bytes 73736 | tf_op jit(solution)/shard_map/ppermute | solution.py:21
  15.9 3.9 %fusion.6 = bf16[4,1024,32]{1,2,0:T(8,128)(2,1)S(1)} fusion(bf16[4,32,1024]{2,1,0:T(8,128)(2,1)} %param.12, s32[4,1024]{1,0:T(4,128)} %param.14), kind=kOutput, calls=%fused_computation.24 | convolution fusion | flops 272760832 | bytes 540672 | tf_op jit(solution)/shard_map/dot_general | solution.py:88
  20.0 3.0 %collective-permute-start.1 = (bf16[2,32,1024]{2,1,0:T(8,128)(2,1)S(1)}, bf16[2,32,1024]{2,1,0:T(8,128)(2,1)S(1)}, u32[]{:S(2)}, u32[]{:S(2)}) collective-permute-start(bf16[2,32,1024]{2,1,0:T(8,128)(2,1)S(1)} %slice.597), channel_id=1, source_target_pairs={{1,0},{2,1},{3,2},{4,3},{5,4},{6,5},{7,6},{8,7},{9,8},{10,9},{11,1... | collective-permute-start | bytes 393224 | tf_op jit(solution)/shard_map/ppermute | solution.py:21
  23.0 0.5 fusion.23
  23.5 0.2 bitcast_convert_fusion
  23.9 0.7 broadcast_in_dim.78
  24.6 3.4 %all-to-all-start = ((f32[4,2,32,256]{3,2,1,0:T(8,128)}), f32[4,2,32,256]{3,2,1,0:T(8,128)S(1)}, u32[]{:S(2)}, u32[]{:S(2)}) async-start(f32[4,2,32,256]{3,2,1,0:T(8,128)} %broadcast_in_dim.78), calls=%async_computation | async-start | bytes 524288 | tf_op jit(solution)/shard_map/all_to_all | solution.py:46
  28.2 0.5 iota_compare_fusion.7
  28.7 0.7 slice.520
  29.4 0.7 fusion.123
  31.6 0.7 fusion.124
  36.1 0.6 pad_clamp_fusion
  36.7 1.1 constant_dynamic-slice_fusion.5
  37.9 0.7 slice_reduce_fusion.5
  38.5 0.6 copy.32
  39.2 4.3 %multiply_convert_fusion.11 = bf16[1024,1024]{1,0:T(8,128)(2,1)} fusion(f32[1024]{0:T(1024)S(1)} %bitcast.361, f32[1024]{0:T(1024)S(1)} %bitcast.362, f32[1024]{0:T(1024)S(1)} %bitcast.363, f32[]{:T(128)S(6)} %copy.46), kind=kLoop, calls=%fused_computation.17 | loop fusion | flops 14680064 | bytes 2109444 | tf_op jit(solution)/shard_map/convert_element_type | solution.py:61
  43.4 7.6 %multiply_convert_fusion.9 = (bf16[1024,1024]{1,0:T(8,128)(2,1)}, bf16[1024,1024]{1,0:T(8,128)(2,1)}) fusion(f32[1024]{0:T(1024)S(1)} %bitcast.347, f32[1024]{0:T(1024)S(1)} %bitcast.348, f32[1024]{0:T(1024)S(1)} %bitcast.346, f32[]{:T(128)S(6)} %copy.46, f32[1024]{0:T(1024)S(1)} %bitcast.349, f32[1024]{0:T(1024)S(1)} %bitcast.350, f32[1024]{0:T(1024)S(1)} %bitcast.351), kind=kLoop, calls=%fused_computation.15 | loop fusion | flops 29360128 | bytes 4218884 | tf_op jit(solution)/shard_map/convert_element_type | solution.py:61
  51.0 3.3 %convolution_multiply_fusion.16 = f32[32,1024]{1,0:T(8,128)} fusion(bf16[1024,1024]{1,0:T(8,128)(2,1)} %multiply_convert_fusion.11, f32[]{:T(128)} %bitcast.61, bf16[4,32,1024]{2,1,0:T(8,128)(2,1)S(1)} %bitcast.289), kind=kOutput, calls=%fused_computation.60 | convolution fusion | flops 67141632 | bytes 2293764 | tf_op jit(solution)/shard_map/dot_general | solution.py:124
  54.4 1.3 constant_dynamic-slice_fusion.1
  55.8 0.6 stack.89
  56.4 0.5 compare_and_fusion
  56.9 3.5 %convolution_multiply_fusion.13 = f32[32,1024]{1,0:T(8,128)} fusion(bf16[1024,1024]{1,0:T(8,128)(2,1)} %get-tuple-element.60, f32[]{:T(128)} %bitcast.114, bf16[4,32,1024]{2,1,0:T(8,128)(2,1)S(1)} %bitcast.290), kind=kOutput, calls=%fused_computation.55 | convolution fusion | flops 67141632 | bytes 2293764 | tf_op jit(solution)/shard_map/dot_general | solution.py:124
  60.4 1.1 convolution_multiply_fusion.9
  61.6 0.9 broadcast_in_dim.80
  62.5 3.7 %all-to-all-start.1 = ((f32[4,5,32,256]{3,2,1,0:T(8,128)}), f32[4,5,32,256]{3,2,1,0:T(8,128)S(1)}, u32[]{:S(2)}, u32[]{:S(2)}) async-start(f32[4,5,32,256]{3,2,1,0:T(8,128)} %broadcast_in_dim.80), calls=%async_computation.1 | async-start | bytes 1310720 | tf_op jit(solution)/shard_map/all_to_all | solution.py:46
  66.2 10.1 %multiply_convert_fusion = (bf16[1024,1024]{1,0:T(8,128)(2,1)S(1)}, bf16[1024,1024]{1,0:T(8,128)(2,1)S(1)}, bf16[1024,1024]{1,0:T(8,128)(2,1)S(1)}) fusion(f32[1024]{0:T(1024)S(1)} %bitcast.353, f32[1024]{0:T(1024)S(1)} %bitcast.354, f32[1024]{0:T(1024)S(1)} %bitcast.352, f32[1024]{0:T(1024)S(1)} %bitcast.359, f32[1024]{0:T(1024)S(1)} %bitcast.358, ...), kind=kLoop, calls=%fused_computation.6 | loop fusion | flops 44040192 | bytes 6328324 | tf_op jit(solution)/shard_map/convert_element_type | solution.py:61
  76.3 1.1 convolution_bitcast_fusion.2
  77.4 1.1 convolution_bitcast_fusion.1
  78.6 1.0 convolution_multiply_fusion.4
  79.6 2.1 %fusion.17 = f32[32,1024]{1,0:T(8,128)} fusion(f32[32,1024]{1,0:T(8,128)S(1)} %convolution_multiply_fusion.9, bf16[1024,1024]{1,0:T(8,128)(2,1)S(1)} %get-tuple-element.58, f32[]{:T(128)} %bitcast.127, bf16[2,32,1024]{2,1,0:T(8,128)(2,1)S(1)} %collective-permute-done.1), kind=kOutput, calls=%fused_computation.47 | convolution fusion | flops 67174400 | bytes 2424836 | tf_op jit(solution)/shard_map/dot_general | solution.py:136
  81.7 2.0 %fusion.12 = f32[32,1024]{1,0:T(8,128)} fusion(f32[32,1024]{1,0:T(8,128)S(1)} %convolution_multiply_fusion.4, bf16[1024,1024]{1,0:T(8,128)(2,1)S(1)} %get-tuple-element.57, f32[]{:T(128)} %bitcast.134, bf16[2,32,1024]{2,1,0:T(8,128)(2,1)S(1)} %collective-permute-done.1), kind=kOutput, calls=%fused_computation.37 | convolution fusion | flops 67174400 | bytes 2424836 | tf_op jit(solution)/shard_map/dot_general | solution.py:136
  83.7 0.7 copy.27
  84.5 1.2 broadcast_in_dim.82
  85.7 3.5 %all-to-all-start.2 = ((f32[4,9,32,256]{3,2,1,0:T(8,128)}), f32[4,9,32,256]{3,2,1,0:T(8,128)S(1)}, u32[]{:S(2)}, u32[]{:S(2)}) async-start(f32[4,9,32,256]{3,2,1,0:T(8,128)} %broadcast_in_dim.82), calls=%async_computation.2 | async-start | bytes 2359296 | tf_op jit(solution)/shard_map/all_to_all | solution.py:46
  89.3 1.1 fusion.119
  90.3 3.3 %multiply_convert_fusion.8 = bf16[1024,1024]{1,0:T(8,128)(2,1)S(1)} fusion(f32[1024]{0:T(1024)S(1)} %bitcast.344, f32[1024]{0:T(1024)S(1)} %bitcast.340, f32[1024]{0:T(1024)S(1)} %bitcast.343, f32[1024]{0:T(1024)S(1)} %bitcast.341, f32[1024]{0:T(1024)S(1)} %bitcast.345, f32[1024]{0:T(1024)S(1)} %bitcast.342, f32[]{:T(128)S(6)} %copy.46), kind=kLoop, calls=%fused_computation.14 | loop fusion | flops 14680064 | bytes 2121732 | tf_op jit(solution)/shard_map/convert_element_type | solution.py:61
  93.6 6.7 %multiply_convert_fusion.6 = (bf16[1024,1024]{1,0:T(8,128)(2,1)S(1)}, bf16[1024,1024]{1,0:T(8,128)(2,1)S(1)}) fusion(f32[1024]{0:T(1024)S(1)} %bitcast.332, f32[1024]{0:T(1024)S(1)} %bitcast.334, f32[1024]{0:T(1024)S(1)} %bitcast.333, f32[1024]{0:T(1024)S(1)} %bitcast.336, f32[1024]{0:T(1024)S(1)} %bitcast.331, f32[1024]{0:T(1024)S(1)} %bitcast.338, ...), kind=kLoop, calls=%fused_computation.12 | loop fusion | flops 29360128 | bytes 4231172 | tf_op jit(solution)/shard_map/convert_element_type | solution.py:61
  100.3 0.5 convolution_bitcast_fusion
  100.8 0.4 copy-done.9
  101.2 0.8 pad_maximum_fusion.1
  102.0 3.1 %collective-permute-start.2 = (f32[3,32,1024]{2,1,0:T(8,128)}, f32[3,32,1024]{2,1,0:T(8,128)}, u32[]{:S(2)}, u32[]{:S(2)}) collective-permute-start(f32[3,32,1024]{2,1,0:T(8,128)} %pad_maximum_fusion.1), channel_id=1, source_target_pairs={{0,1},{1,2},{2,3},{3,4},{4,5},{5,6},{6,7},{7,8},{8,9},{9,10},{10,1... | collective-permute-start | bytes 1179656 | tf_op jit(solution)/shard_map/ppermute | solution.py:183
  105.2 2.1 %fusion.22 = f32[32,1024]{1,0:T(8,128)} fusion(f32[32,1024]{1,0:T(8,128)S(1)} %copy-done.11, bf16[1024,1024]{1,0:T(8,128)(2,1)S(1)} %get-tuple-element.51, f32[]{:T(128)} %bitcast.78, bf16[4,32,1024]{2,1,0:T(8,128)(2,1)S(1)} %bitcast.296), kind=kOutput, calls=%fused_computation.59 | convolution fusion | flops 67174400 | bytes 2424836 | tf_op jit(solution)/shard_map/dot_general | solution.py:136
  107.2 1.1 fusion.20
  108.4 2.1 %fusion.19 = f32[32,1024]{1,0:T(8,128)} fusion(f32[32,1024]{1,0:T(8,128)S(1)} %fusion.20, bf16[1024,1024]{1,0:T(8,128)(2,1)S(1)} %get-tuple-element.61, f32[]{:T(128)} %bitcast.118, bf16[4,32,1024]{2,1,0:T(8,128)(2,1)S(1)} %bitcast.298), kind=kOutput, calls=%fused_computation.52 | convolution fusion | flops 67174400 | bytes 2424836 | tf_op jit(solution)/shard_map/dot_general | solution.py:136
  110.5 1.7 %fusion.16 = f32[32,1024]{1,0:T(8,128)} fusion(f32[32,1024]{1,0:T(8,128)S(1)} %copy-done.15, bf16[1024,1024]{1,0:T(8,128)(2,1)S(1)} %get-tuple-element.61, f32[]{:T(128)} %bitcast.128, bf16[4,32,1024]{2,1,0:T(8,128)(2,1)S(1)} %bitcast.299), kind=kOutput, calls=%fused_computation.45 | convolution fusion | flops 67174400 | bytes 2424836 | tf_op jit(solution)/shard_map/dot_general | solution.py:131
  112.2 2.0 %fusion.11 = f32[32,1024]{1,0:T(8,128)} fusion(f32[32,1024]{1,0:T(8,128)S(1)} %copy-done.14, bf16[1024,1024]{1,0:T(8,128)(2,1)S(1)} %multiply_convert_fusion.8, f32[]{:T(128)} %bitcast.136, bf16[2,32,1024]{2,1,0:T(8,128)(2,1)S(1)} %copy-done.19), kind=kOutput, calls=%fused_computation.35 | convolution fusion | flops 67174400 | bytes 2424836 | tf_op jit(solution)/shard_map/dot_general | solution.py:136
  114.2 1.6 fusion.118
  115.8 0.7 broadcast_in_dim.83
  116.4 6.8 %all-to-all-start.3 = ((bf16[8,32,256]{2,1,0:T(8,128)(2,1)}), bf16[8,32,256]{2,1,0:T(8,128)(2,1)}, u32[]{:S(2)}, u32[]{:S(2)}) async-start(bf16[8,32,256]{2,1,0:T(8,128)(2,1)} %broadcast_in_dim.83), calls=%async_computation.3 | async-start | bytes 262144 | tf_op jit(solution)/shard_map/all_to_all | solution.py:46
  123.2 11.4 %multiply_convert_fusion.3 = (bf16[1024,1024]{1,0:T(8,128)(2,1)}, bf16[1024,1024]{1,0:T(8,128)(2,1)}, bf16[1024,1024]{1,0:T(8,128)(2,1)}) fusion(f32[1024]{0:T(1024)} %bitcast.320, f32[1024]{0:T(1024)} %bitcast.321, f32[1024]{0:T(1024)} %bitcast.319, f32[1024]{0:T(1024)} %bitcast.325, f32[1024]{0:T(1024)} %bitcast.327, f32[1024]{0:T(1024)} %bitcast.329, ...), kind=kLoop, calls=%fused_computation.9 | loop fusion | flops 44040192 | bytes 6340612 | tf_op jit(solution)/shard_map/convert_element_type | solution.py:61
  134.9 0.7 gather_fusion
  135.5 0.8 fusion.65
  136.4 3.1 %fusion.15 = f32[32,1024]{1,0:T(8,128)S(1)} fusion(f32[32,1024]{1,0:T(8,128)} %fusion.16, bf16[1024,1024]{1,0:T(8,128)(2,1)} %get-tuple-element.64, f32[]{:T(128)} %bitcast.129, bf16[4,32,1024]{2,1,0:T(8,128)(2,1)S(1)} %bitcast.300), kind=kOutput, calls=%fused_computation.43 | convolution fusion | flops 67174400 | bytes 2424836 | tf_op jit(solution)/shard_map/dot_general | solution.py:136
  139.5 1.2 fusion.14
  140.8 1.2 fusion.10
  142.0 3.5 %fusion.59 = f32[1,32,1024]{2,1,0:T(8,128)S(1)} fusion(f32[3,32,1024]{2,1,0:T(8,128)} %collective-permute-done.2, f32[32,1024]{1,0:T(8,128)S(1)} %copy-done.16, bf16[1024,1024]{1,0:T(8,128)(2,1)S(1)} %copy-done.2, f32[]{:T(128)} %bitcast.110, f32[]{:T(128)} %bitcast.108, f32[]{:T(128)} %bitcast.92, bf16[4,32,1024]{2,1,0:T(8,128)(2,1)S(1)} %bitcast.303), kind=kOutput, calls=%fused_computation.100 | convolution fusion | flops 67305472 | bytes 2686988 | tf_op jit(solution)/shard_map/dot_general | solution.py:136
  145.6 2.8 %fusion.56 = f32[1,32,1024]{2,1,0:T(8,128)S(1)} fusion(f32[3,32,1024]{2,1,0:T(8,128)} %collective-permute-done.2, f32[32,1024]{1,0:T(8,128)S(1)} %copy-done.13, bf16[1024,1024]{1,0:T(8,128)(2,1)S(1)} %copy-done.1, f32[]{:T(128)} %bitcast.121, f32[]{:T(128)} %bitcast.120, bf16[4,32,1024]{2,1,0:T(8,128)(2,1)S(1)} %bitcast.304), kind=kOutput, calls=%fused_computation.96 | convolution fusion | flops 67239936 | bytes 2555912 | tf_op jit(solution)/shard_map/dot_general | solution.py:136
  148.5 1.1 fusion.9
  149.6 1.0 select_bitcast_fusion
  150.6 2.5 %fusion.26 = f32[32,256]{1,0:T(8,128)} fusion(bf16[32,2048]{1,0:T(8,128)(2,1)S(1)} %bitcast.311, f32[256]{0:T(256)S(1)} %bitcast.367, f32[2048]{0:T(1024)S(1)} %bitcast.317, f32[256]{0:T(256)S(1)} %bitcast.368, f32[2048]{0:T(1024)S(1)} %bitcast.318, f32[256]{0:T(256)S(1)} %bitcast.369, f32[2048]{0:T(1024)S(1)} %bitcast.316, f32[]{:T(128)S(6)} %copy.46, ...), kind=kOutput, calls=%fused_computation.69 | convolution fusion | flops 45096960 | bytes 322564 | tf_op jit(solution)/shard_map/dot_general | solution.py:233
  153.1 2.2 %fusion.27 = bf16[32,256,1]{1,0,2:T(8,128)(2,1)S(1)} fusion(f32[32,256]{1,0:T(8,128)} %fusion.26, bf16[32,1536]{1,0:T(8,128)(2,1)S(1)} %bitcast.314, f32[256]{0:T(256)} %bitcast.366, f32[1536]{0:T(1024)S(1)} %copy-done.27, f32[256]{0:T(256)} %bitcast.365, f32[1536]{0:T(1024)} %get-tuple-element.69, f32[256]{0:T(256)} %bitcast.364, f32[1536]{0:T(1024)S(1)} %copy-done.26, ...), kind=kOutput, calls=%fused_computation.70 | convolution fusion | flops 30687232 | bytes 168964 | tf_op jit(solution)/shard_map/dot_general | solution.py:231
  155.3 1.6 fusion.5
  156.9 4.9 %fusion.7 = bf16[4,32,1024]{2,1,0:T(8,128)(2,1)} fusion(bf16[4,32,1024]{2,1,0:T(8,128)(2,1)} %fusion.5, s32[4,1024]{1,0:T(4,128)S(1)} %copy-done.33), kind=kOutput, calls=%fused_computation.25 | convolution fusion | flops 272760832 | bytes 540672 | tf_op jit(solution)/shard_map/dot_general | solution.py:247
  (106 shorter events, 1.1 us)
Async XLA Ops:
  0.0 23.0 %copy-start = (bf16[4,1024,256]{2,1,0:T(8,128)(2,1)S(1)}, bf16[4,1024,256]{2,1,0:T(8,128)(2,1)}, u32[]{:S(2)}) copy-start(bf16[4,1024,256]{2,1,0:T(8,128)(2,1)} %param.15) | copy-start | bytes 6291460
  1.0 60.6 %collective-permute-start = (f32[2,3,1024]{2,0,1:T(2,128)S(1)}, f32[2,3,1024]{2,0,1:T(2,128)S(1)}, u32[]{:S(2)}, u32[]{:S(2)}) collective-permute-start(f32[2,3,1024]{2,0,1:T(2,128)S(1)} %slice.482), channel_id=1, source_target_pairs={{1,0},{2,1},{3,2},{4,3},{5,4},{6,5},{7,6},{8,7},{9,8},{10,9},{11,1... | collective-permute-start | bytes 73736 | tf_op jit(solution)/shard_map/ppermute | solution.py:21
  19.9 3.6 %copy-start.5 = (bf16[1,4,256,256]{3,2,1,0:T(8,128)(2,1)S(1)}, bf16[1,4,256,256]{3,2,1,0:T(8,128)(2,1)}, u32[]{:S(2)}) copy-start(bf16[1,4,256,256]{3,2,1,0:T(8,128)(2,1)} %param.16) | copy-start | bytes 1572868
  19.9 3.8 %copy-start.20 = (bf16[1,256,256]{2,1,0:T(8,128)(2,1)S(1)}, bf16[1,256,256]{2,1,0:T(8,128)(2,1)}, u32[]{:S(2)}) copy-start(bf16[1,256,256]{2,1,0:T(8,128)(2,1)} %param.17) | copy-start | bytes 393220
  19.9 8.8 %copy-start.28 = (s32[4,5]{1,0:T(4,128)S(1)}, s32[4,5]{1,0:T(4,128)}, u32[]{:S(2)}) copy-start(s32[4,5]{1,0:T(4,128)} %param.20) | copy-start | bytes 244
  19.9 11.7 %copy-start.24 = (s32[1,9]{1,0:T(1,128)S(1)}, s32[1,9]{1,0:T(1,128)}, u32[]{:S(2)}) copy-start(s32[1,9]{1,0:T(1,128)} %param.21) | copy-start | bytes 112
  20.0 18.6 %copy-start.22 = (f32[8,3,256]{2,0,1:T(8,128)S(1)}, f32[8,3,256]{2,0,1:T(8,128)}, u32[]{:S(2)}) copy-start(f32[8,3,256]{2,0,1:T(8,128)} %param.19) | copy-start | bytes 73732
  20.0 19.2 %copy-start.8 = (f32[4,3,1024]{2,0,1:T(4,128)S(1)}, f32[4,3,1024]{2,0,1:T(4,128)}, u32[]{:S(2)}) copy-start(f32[4,3,1024]{2,0,1:T(4,128)} %param.13) | copy-start | bytes 147460
  20.0 41.6 %collective-permute-start.1 = (bf16[2,32,1024]{2,1,0:T(8,128)(2,1)S(1)}, bf16[2,32,1024]{2,1,0:T(8,128)(2,1)S(1)}, u32[]{:S(2)}, u32[]{:S(2)}) collective-permute-start(bf16[2,32,1024]{2,1,0:T(8,128)(2,1)S(1)} %slice.597), channel_id=1, source_target_pairs={{1,0},{2,1},{3,2},{4,3},{5,4},{6,5},{7,6},{8,7},{9,8},{10,9},{11,1... | collective-permute-start | bytes 393224 | tf_op jit(solution)/shard_map/ppermute | solution.py:21
  24.6 36.9 %all-to-all-start = ((f32[4,2,32,256]{3,2,1,0:T(8,128)}), f32[4,2,32,256]{3,2,1,0:T(8,128)S(1)}, u32[]{:S(2)}, u32[]{:S(2)}) async-start(f32[4,2,32,256]{3,2,1,0:T(8,128)} %broadcast_in_dim.78), calls=%async_computation | async-start | bytes 524288 | tf_op jit(solution)/shard_map/all_to_all | solution.py:46
  56.4 4.1 %copy-start.4 = (bf16[1024,1024]{1,0:T(8,128)(2,1)S(1)}, bf16[1024,1024]{1,0:T(8,128)(2,1)}, u32[]{:S(2)}) copy-start(bf16[1024,1024]{1,0:T(8,128)(2,1)} %get-tuple-element.63) | copy-start | bytes 6291460
  61.6 14.7 %copy-start.23 = (f32[2,3,1024]{2,0,1:T(2,128)}, f32[2,3,1024]{2,0,1:T(2,128)S(1)}, u32[]{:S(2)}) copy-start(f32[2,3,1024]{2,0,1:T(2,128)S(1)} %collective-permute-done) | copy-start | bytes 73732
  61.6 20.1 %copy-start.18 = (bf16[2,32,1024]{2,1,0:T(8,128)(2,1)}, bf16[2,32,1024]{2,1,0:T(8,128)(2,1)S(1)}, u32[]{:S(2)}) copy-start(bf16[2,32,1024]{2,1,0:T(8,128)(2,1)S(1)} %collective-permute-done.1) | copy-start | bytes 393220
  62.5 21.1 %all-to-all-start.1 = ((f32[4,5,32,256]{3,2,1,0:T(8,128)}), f32[4,5,32,256]{3,2,1,0:T(8,128)S(1)}, u32[]{:S(2)}, u32[]{:S(2)}) async-start(f32[4,5,32,256]{3,2,1,0:T(8,128)} %broadcast_in_dim.80), calls=%async_computation.1 | async-start | bytes 1310720 | tf_op jit(solution)/shard_map/all_to_all | solution.py:46
  85.7 28.4 %all-to-all-start.2 = ((f32[4,9,32,256]{3,2,1,0:T(8,128)}), f32[4,9,32,256]{3,2,1,0:T(8,128)S(1)}, u32[]{:S(2)}, u32[]{:S(2)}) async-start(f32[4,9,32,256]{3,2,1,0:T(8,128)} %broadcast_in_dim.82), calls=%async_computation.2 | async-start | bytes 2359296 | tf_op jit(solution)/shard_map/all_to_all | solution.py:46
  100.3 0.9 copy-start.9
  100.3 1.0 copy-start.10
  100.3 4.9 %copy-start.11 = (f32[32,1024]{1,0:T(8,128)S(1)}, f32[32,1024]{1,0:T(8,128)}, u32[]{:S(2)}) copy-start(f32[32,1024]{1,0:T(8,128)} %convolution_multiply_fusion.16) | copy-start | bytes 393220
  101.2 6.0 %copy-start.12 = (f32[32,1024]{1,0:T(8,128)S(1)}, f32[32,1024]{1,0:T(8,128)}, u32[]{:S(2)}) copy-start(f32[32,1024]{1,0:T(8,128)} %convolution_multiply_fusion.13) | copy-start | bytes 393220
  102.0 40.0 %collective-permute-start.2 = (f32[3,32,1024]{2,1,0:T(8,128)}, f32[3,32,1024]{2,1,0:T(8,128)}, u32[]{:S(2)}, u32[]{:S(2)}) collective-permute-start(f32[3,32,1024]{2,1,0:T(8,128)} %pad_maximum_fusion.1), channel_id=1, source_target_pairs={{0,1},{1,2},{2,3},{3,4},{4,5},{5,6},{6,7},{7,8},{8,9},{9,10},{10,1... | collective-permute-start | bytes 1179656 | tf_op jit(solution)/shard_map/ppermute | solution.py:183
  107.2 3.2 %copy-start.15 = (f32[32,1024]{1,0:T(8,128)S(1)}, f32[32,1024]{1,0:T(8,128)}, u32[]{:S(2)}) copy-start(f32[32,1024]{1,0:T(8,128)} %fusion.17) | copy-start | bytes 393220
  108.4 3.8 %copy-start.14 = (f32[32,1024]{1,0:T(8,128)S(1)}, f32[32,1024]{1,0:T(8,128)}, u32[]{:S(2)}) copy-start(f32[32,1024]{1,0:T(8,128)} %fusion.12) | copy-start | bytes 393220
  108.4 3.8 %copy-start.19 = (bf16[2,32,1024]{2,1,0:T(8,128)(2,1)S(1)}, bf16[2,32,1024]{2,1,0:T(8,128)(2,1)}, u32[]{:S(2)}) copy-start(bf16[2,32,1024]{2,1,0:T(8,128)(2,1)} %copy-done.18) | copy-start | bytes 393220
  116.4 33.1 %all-to-all-start.3 = ((bf16[8,32,256]{2,1,0:T(8,128)(2,1)}), bf16[8,32,256]{2,1,0:T(8,128)(2,1)}, u32[]{:S(2)}, u32[]{:S(2)}) async-start(bf16[8,32,256]{2,1,0:T(8,128)(2,1)} %broadcast_in_dim.83), calls=%async_computation.3 | async-start | bytes 262144 | tf_op jit(solution)/shard_map/all_to_all | solution.py:46
  123.2 11.5 %copy-start.7 = (bf16[4,4,32,256]{3,2,0,1:T(8,128)(2,1)S(1)}, bf16[4,4,32,256]{3,2,0,1:T(8,128)(2,1)}, u32[]{:S(2)}) copy-start(bf16[4,4,32,256]{3,2,0,1:T(8,128)(2,1)} %copy.27) | copy-start | bytes 786436
  135.5 4.0 %copy-start.2 = (bf16[1024,1024]{1,0:T(8,128)(2,1)S(1)}, bf16[1024,1024]{1,0:T(8,128)(2,1)}, u32[]{:S(2)}) copy-start(bf16[1024,1024]{1,0:T(8,128)(2,1)} %get-tuple-element.54) | copy-start | bytes 6291460
  136.4 4.3 %copy-start.3 = (bf16[1024,1024]{1,0:T(8,128)(2,1)S(1)}, bf16[1024,1024]{1,0:T(8,128)(2,1)}, u32[]{:S(2)}) copy-start(bf16[1024,1024]{1,0:T(8,128)(2,1)} %get-tuple-element.64) | copy-start | bytes 6291460
  136.4 4.3 %copy-start.17 = (f32[32,1024]{1,0:T(8,128)S(1)}, f32[32,1024]{1,0:T(8,128)}, u32[]{:S(2)}) copy-start(f32[32,1024]{1,0:T(8,128)} %fusion.11) | copy-start | bytes 393220
  139.5 2.5 %copy-start.16 = (f32[32,1024]{1,0:T(8,128)S(1)}, f32[32,1024]{1,0:T(8,128)}, u32[]{:S(2)}) copy-start(f32[32,1024]{1,0:T(8,128)} %fusion.22) | copy-start | bytes 393220
  140.7 4.8 %copy-start.1 = (bf16[1024,1024]{1,0:T(8,128)(2,1)S(1)}, bf16[1024,1024]{1,0:T(8,128)(2,1)}, u32[]{:S(2)}) copy-start(bf16[1024,1024]{1,0:T(8,128)(2,1)} %get-tuple-element.62) | copy-start | bytes 6291460
  140.8 4.8 %copy-start.13 = (f32[32,1024]{1,0:T(8,128)S(1)}, f32[32,1024]{1,0:T(8,128)}, u32[]{:S(2)}) copy-start(f32[32,1024]{1,0:T(8,128)} %fusion.19) | copy-start | bytes 393220
  145.6 4.0 %copy-start.32 = (pred[8]{0:T(512)(128)(4,1)S(1)}, pred[8]{0:T(512)(128)(4,1)}, u32[]{:S(2)}) copy-start(pred[8]{0:T(512)(128)(4,1)} %iota_compare_fusion.7) | copy-start | bytes 28
  148.4 2.1 %copy-start.21 = (bf16[1,256,256]{2,1,0:T(8,128)(2,1)S(1)}, bf16[1,256,256]{2,1,0:T(8,128)(2,1)}, u32[]{:S(2)}) copy-start(bf16[1,256,256]{2,1,0:T(8,128)(2,1)} %param.17) | copy-start | bytes 393220
  148.4 2.1 %copy-start.25 = (f32[1,2,8,128]{3,1,2,0:T(2,128)S(1)}, f32[1,2,8,128]{3,1,2,0:T(2,128)}, u32[]{:S(2)}) copy-start(f32[1,2,8,128]{3,1,2,0:T(2,128)} %copy.32) | copy-start | bytes 24580
  148.4 2.1 %copy-start.29 = (f32[1,1,256]{2,0,1:T(1,128)S(1)}, f32[1,1,256]{2,0,1:T(1,128)}, u32[]{:S(2)}) copy-start(f32[1,1,256]{2,0,1:T(1,128)} %get-tuple-element.175) | copy-start | bytes 3076
  148.4 2.1 %copy-start.30 = (f32[1,1,256]{2,0,1:T(1,128)S(1)}, f32[1,1,256]{2,0,1:T(1,128)}, u32[]{:S(2)}) copy-start(f32[1,1,256]{2,0,1:T(1,128)} %get-tuple-element.176) | copy-start | bytes 3076
  148.5 2.1 %copy-start.31 = (f32[1,1,256]{2,0,1:T(1,128)S(1)}, f32[1,1,256]{2,0,1:T(1,128)}, u32[]{:S(2)}) copy-start(f32[1,1,256]{2,0,1:T(1,128)} %get-tuple-element.177) | copy-start | bytes 3076
  150.6 2.5 %copy-start.26 = (f32[1536]{0:T(1024)S(1)}, f32[1536]{0:T(1024)}, u32[]{:S(2)}) copy-start(f32[1536]{0:T(1024)} %get-tuple-element.67) | copy-start | bytes 18436
  150.6 2.5 %copy-start.27 = (f32[1536]{0:T(1024)S(1)}, f32[1536]{0:T(1024)}, u32[]{:S(2)}) copy-start(f32[1536]{0:T(1024)} %get-tuple-element.68) | copy-start | bytes 18436
  153.1 2.2 %copy-start.6 = (bf16[1,4,256,256]{3,2,1,0:T(8,128)(2,1)S(1)}, bf16[1,4,256,256]{3,2,1,0:T(8,128)(2,1)}, u32[]{:S(2)}) copy-start(bf16[1,4,256,256]{3,2,1,0:T(8,128)(2,1)} %param.16) | copy-start | bytes 1572868
  155.3 1.6 copy-start.33
